TPU v7x, 256 devices: a whole 4x4x8 slice. The times are simulated.
256 devices in a mesh: dp: 64 (over x, z, core), mp: 4 (over y).
Axes of the slice: x: 4, y: 4, z: 8, core: 2. Of those that a mesh axis runs over, the one named last changes fastest.
Arguments:
- attn: bfloat16 [2, 4096, 2048], P(None, 'dp', 'mp'), may hold values from -6 to 6
- resid: bfloat16 [2, 4096, 4096], P(None, 'dp', 'mp'), may hold values from -6 to 6
- w_out: bfloat16 [4096, 2048], P('dp', 'mp'), may hold values from -0.125 to 0.125
- gain: float32 [4096], P('mp'), may hold values from 0.1 to 1.9
- neg_owner: int32 [4096, 31], P('dp'), may hold values from 0 to 63, as said below
- neg_local: int32 [4096, 31], P('dp'), may hold values from 0 to 63
Outputs:
- attn_grad: bfloat16 [2, 4096, 2048], P(None, 'dp', 'mp')
- weight_grad: float32 [4096, 2048], P('dp', 'mp')
- gain_grad: float32 [4096], P('mp')
Inputs may be any that keep to these rules, and one draw needn't show every extreme that they name: `neg_owner`: among the 64 queries of one index of dp (aligned blocks of rows), no owner is named more than 62 times, and some owner exactly 62 times.
All inputs are finite; a program needn't handle non-finite values.
Results may differ from a plain program's by a relative error of at most 0.0052.
Values may be sent and summed in bfloat16 or wider, within the bound.
No kernel may reach another device: no remote copies, remote signals or barrier semaphores. Data moves between devices by JAX's collectives and lax.ppermute only.
A program may use at most 128 MiB of HBM per device.

v0:
```python
import jax
import jax.numpy as jnp
import numpy as np
from jax import lax
from jax.sharding import Mesh, PartitionSpec as P

TAU = 0.05
LOSS_SCALE = 32.0
EPS = 1e-06
XZ = ("x", "z")
DP = ("x", "z", "c")


def ring_collect(v, name, n):
    if n == 1:
        return v[None]
    me = lax.axis_index(name)
    fwd = [(i, (i + 1) % n) for i in range(n)]
    bwd = [(i, (i - 1) % n) for i in range(n)]
    out = jnp.zeros((n,) + v.shape, v.dtype)
    out = lax.dynamic_update_index_in_dim(out, v, me, 0)
    if n == 2:
        pair = jnp.stack([v, lax.ppermute(v, name, fwd)])
        return jnp.where(me == 0, pair, pair[::-1])
    n_fwd = n // 2
    n_bwd = (n - 1) // 2
    left = right = v
    for step in range(1, n_fwd + 1):
        if step > n_bwd and v.size * v.dtype.itemsize < (1 << 19):
            left = lax.ppermute(left, name, fwd)
            out = lax.dynamic_update_index_in_dim(out, left, (me - step) % n, 0)
            break
        if step > n_bwd:
            half = v.shape[0] // 2
            got = jnp.concatenate(
                [lax.ppermute(left[:half], name, fwd), lax.ppermute(right[half:], name, bwd)], axis=0
            )
            out = lax.dynamic_update_index_in_dim(out, got, (me - step) % n, 0)
            break
        left = lax.ppermute(left, name, fwd)
        out = lax.dynamic_update_index_in_dim(out, left, (me - step) % n, 0)
        right = lax.ppermute(right, name, bwd)
        out = lax.dynamic_update_index_in_dim(out, right, (me + step) % n, 0)
    return out


def ring_blocks(v, name, n):
    if n == 1:
        return [v]
    fwd = [(i, (i + 1) % n) for i in range(n)]
    bwd = [(i, (i - 1) % n) for i in range(n)]
    if n == 2:
        return [v, lax.ppermute(v, name, fwd)]
    n_fwd = n // 2
    n_bwd = (n - 1) // 2
    blocks = [None] * n
    blocks[0] = v
    left = right = v
    for step in range(1, n_fwd + 1):
        if step > n_bwd and v.size * v.dtype.itemsize >= (1 << 19):
            half = v.shape[0] // 2
            blocks[n - step] = jnp.concatenate(
                [lax.ppermute(left[:half], name, fwd), lax.ppermute(right[half:], name, bwd)], axis=0
            )
            break
        left = lax.ppermute(left, name, fwd)
        blocks[n - step] = left
        if step <= n_bwd:
            right = lax.ppermute(right, name, bwd)
            blocks[step] = right
    return blocks


def gather_rel(v, first="x", second="z"):
    g1 = jnp.stack(ring_blocks(v, first, lax.axis_size(first)))
    g2 = jnp.stack(ring_blocks(g1, second, lax.axis_size(second)))
    return ring_blocks(g2, "c", lax.axis_size("c"))


def gather_dp(v):
    gx = ring_collect(v, "x", lax.axis_size("x"))
    gz = ring_collect(gx, "z", lax.axis_size("z"))
    return ring_collect(gz, "c", lax.axis_size("c"))


def ring_reduce(v, name, n, axis):
    if n == 1:
        return v
    me = lax.axis_index(name)
    fwd = [(i, (i + 1) % n) for i in range(n)]
    bwd = [(i, (i - 1) % n) for i in range(n)]

    def block(j):
        return lax.dynamic_index_in_dim(v, j % n, axis, keepdims=False)

    if n == 2:
        return block(me) + lax.ppermute(block(me + 1), name, fwd)
    n_fwd = n // 2
    n_bwd = (n - 1) // 2
    acc_f = block(me + n_fwd)
    for step in range(1, n_fwd + 1):
        acc_f = lax.ppermute(acc_f, name, fwd) + block(me + n_fwd - step)
    total = acc_f
    if n_bwd > 0:
        acc_b = block(me - n_bwd)
        for step in range(1, n_bwd):
            acc_b = lax.ppermute(acc_b, name, bwd) + block(me - n_bwd + step)
        total = total + lax.ppermute(acc_b, name, bwd)
    return total


def ring_sum(v, name):
    return jnp.sum(ring_collect(v, name, lax.axis_size(name)), axis=0)


def split_bf16(v):
    hi = v.astype(jnp.bfloat16)
    lo = (v - hi.astype(jnp.float32)).astype(jnp.bfloat16)
    return jnp.concatenate([hi, lo], axis=0)


def mm(a, b):
    return jnp.dot(a, b, preferred_element_type=jnp.float32)


def shards(attn, resid, w_out, gain, neg_owner, neg_local):
    n_xz = lax.axis_size("x") * lax.axis_size("z")
    n_c = lax.axis_size("c")
    pairs_here = attn.shape[1]
    heads = attn.shape[2]
    feats = resid.shape[2]
    w_rows = w_out.shape[0]
    total = pairs_here * n_xz * n_c

    n_x = lax.axis_size("x")
    n_z = lax.axis_size("z")
    step_x = (neg_owner // (n_z * n_c) - lax.axis_index("x")) % n_x
    step_z = ((neg_owner // n_c) % n_z - lax.axis_index("z")) % n_z
    step_c = (neg_owner % n_c - lax.axis_index("c")) % n_c
    pos = ((step_c * n_x + step_x) * n_z + step_z) * pairs_here + neg_local
    pos_t = pos.T

    w_z = ring_collect(w_out, "z", n_z)
    w_xz = ring_collect(w_z, "x", n_x)
    weight_full = ring_collect(w_xz, "c", n_c).transpose(1, 2, 0, 3, 4).reshape(-1, heads)
    rows_a = attn.reshape(2 * pairs_here, heads)
    proj_part = lax.dot_general(
        rows_a, weight_full, (((1,), (1,)), ((), ())), preferred_element_type=jnp.float32
    )
    n_mp = lax.axis_size("mp")
    proj = ring_reduce(proj_part.reshape(proj_part.shape[0], n_mp, feats), "mp", n_mp, 1)
    hidden = resid.reshape(2 * pairs_here, feats).astype(jnp.float32) + proj
    normed = hidden * gain
    squares = ring_sum(jnp.sum(normed * normed, axis=1), "mp")
    recip = lax.rsqrt(squares + EPS)[:, None]
    emb = (normed * recip).astype(jnp.bfloat16)
    query = emb[:pairs_here]
    docs = emb[pairs_here:]
    query_f = query.astype(jnp.float32)
    docs_f = docs.astype(jnp.float32)
    q_all = jnp.stack(gather_rel(query, "x", "z")).reshape(total, feats)
    e_all = jnp.stack(gather_rel(docs, "z", "x")).reshape(total, feats)

    all_scores = lax.dot_general(
        query, e_all, (((1,), (1,)), ((), ())), preferred_element_type=jnp.float32
    )
    cols = lax.broadcasted_iota(jnp.int32, (1, 1, total), 2)
    neg_part = jnp.sum(jnp.where(pos[:, :, None] == cols, all_scores[:, None, :], 0.0), axis=2)
    pos_part = jnp.sum(query_f * docs_f, axis=1)
    partial_value = jnp.concatenate([pos_part[:, None], neg_part], axis=1)
    scores = ring_sum(partial_value, "mp") / TAU
    expo = jnp.exp(scores)
    prob = expo / jnp.sum(expo, axis=1, keepdims=True)
    first = (jnp.arange(scores.shape[1]) == 0).astype(jnp.float32)[None, :]
    wts = LOSS_SCALE * (prob - first) / TAU
    wts_neg_t = wts[:, 1:].T
    neg_count = pos.shape[1]
    doc_ids = neg_owner * pairs_here + neg_local
    packed = jnp.concatenate([wts[:, 1:], doc_ids.astype(jnp.float32)], axis=1)
    packed_all_t = jnp.stack(gather_rel(packed)).reshape(total, -1).T
    wts_all_t = packed_all_t[:neg_count]
    ids_all_t = packed_all_t[neg_count:].astype(jnp.int32)

    coef_q = jnp.sum(jnp.where(pos_t[:, :, None] == cols, wts_neg_t[:, :, None], 0.0), axis=0)
    both = mm(split_bf16(coef_q), e_all)
    grad_query = wts[:, 0:1] * docs_f + both[:pairs_here] + both[pairs_here:]

    me = (lax.axis_index("x") * n_z + lax.axis_index("z")) * n_c + lax.axis_index("c")
    own = me * pairs_here + lax.broadcasted_iota(jnp.int32, (1, pairs_here, 1), 1)
    coef_d = jnp.sum(jnp.where(ids_all_t[:, None, :] == own, wts_all_t[:, None, :], 0.0), axis=0)
    both_d = mm(split_bf16(coef_d), q_all)
    grad_docs = wts[:, 0:1] * query_f + both_d[:pairs_here] + both_d[pairs_here:]

    demb = jnp.concatenate([grad_query, grad_docs], axis=0)
    inner = ring_sum(jnp.sum(normed * demb, axis=1), "mp")[:, None]
    dnorm = recip * demb - recip * recip * recip * normed * inner
    gain_grad = jnp.sum(gather_dp(jnp.sum(dnorm * hidden, axis=0)), axis=(0, 1, 2))
    dh = (dnorm * gain).astype(jnp.bfloat16)
    dh_full = ring_collect(dh, "mp", n_mp).transpose(1, 0, 2).reshape(dh.shape[0], -1)
    attn_grad = mm(dh_full, weight_full).astype(jnp.bfloat16).reshape(attn.shape)
    wg_part = lax.dot_general(
        dh_full, rows_a, (((0,), (0,)), ((), ())), preferred_element_type=jnp.float32
    ).reshape(n_x, n_z, n_c, w_rows, heads)
    wg_xz = ring_reduce(wg_part, "c", n_c, 2)
    wg_x = ring_reduce(wg_xz, "z", n_z, 1)
    weight_grad = ring_reduce(wg_x, "x", n_x, 0)
    return (attn_grad, weight_grad, gain_grad)


def split_mesh(mesh):
    grid = mesh.devices
    n_dp, n_mp = grid.shape
    column = grid[:, 0]
    n_x = len({d.coords[0] for d in column})
    n_c = len({d.core_on_chip for d in column})
    n_z = n_dp // (n_x * n_c)
    return Mesh(grid.reshape(n_x, n_z, n_c, n_mp), ("x", "z", "c", "mp"))


def solution(mesh):
    inner_mesh = split_mesh(mesh)
    in_specs = (
        P(None, DP, "mp"),
        P(None, DP, "mp"),
        P(DP, "mp"),
        P("mp"),
        P(DP, None),
        P(DP, None),
    )
    out_specs = (P(None, DP, "mp"), P(DP, "mp"), P("mp"))
    return jax.shard_map(
        shards, mesh=inner_mesh, in_specs=in_specs, out_specs=out_specs, check_vma=False
    )
```

profile of v0, /device:TPU:1, one launch (start us, length us, event | category | flops | bytes accessed | tf_op | source)
XLA Modules:
  0.0 437.4 jit_solution(17981635580821119029)
XLA Ops:
  24.8 5.8 %collective-permute-done.8 = bf16[8,64,512]{2,1,0:T(8,128)(2,1)S(1)} collective-permute-done((bf16[8,64,512]{2,1,0:T(8,128)(2,1)S(1)}, bf16[8,64,512]{2,1,0:T(8,128)(2,1)S(1)}, u32[]{:S(2)}, u32[]{:S(2)}) %collective-permute-start.8) | collective-permute-done | bytes 524320 | tf_op jit(solution)/shard_map/ppermute | solution.py:42
  42.4 8.5 %collective-permute-start.11 = (bf16[4,8,64,512]{3,2,1,0:T(8,128)(2,1)S(1)}, bf16[4,8,64,512]{3,2,1,0:T(8,128)(2,1)}, u32[]{:S(2)}, u32[]{:S(2)}) collective-permute-start(bf16[4,8,64,512]{3,2,1,0:T(8,128)(2,1)S(1)} %fusion.8), channel_id=1, source_target_pairs={{0,4},{4,0},{1,5},{5,1},{2,6},{6,2},{3,7},{7,3},{8,12},{12,8},{9,1... | collective-permute-start | bytes 6291464 | tf_op jit(solution)/shard_map/ppermute | solution.py:23
  64.5 11.4 %collective-permute-done.12 = f32[128,1024]{1,0:T(8,128)S(1)} collective-permute-done((f32[128,1024]{1,0:T(8,128)}, f32[128,1024]{1,0:T(8,128)S(1)}, u32[]{:S(2)}, u32[]{:S(2)}) %collective-permute-start.12) | collective-permute-done | bytes 524320 | tf_op jit(solution)/shard_map/ppermute | solution.py:102
  76.3 13.2 %collective-permute-done.13 = f32[128,1024]{1,0:T(8,128)S(1)} collective-permute-done((f32[128,1024]{1,0:T(8,128)S(1)}, f32[128,1024]{1,0:T(8,128)S(1)}, u32[]{:S(2)}, u32[]{:S(2)}) %collective-permute-start.13) | collective-permute-done | bytes 524320 | tf_op jit(solution)/shard_map/ppermute | solution.py:102
  109.8 5.9 %collective-permute-done.23 = bf16[64,1024]{1,0:T(8,128)(2,1)S(1)} collective-permute-done((bf16[64,1024]{1,0:T(8,128)(2,1)S(1)}, bf16[64,1024]{1,0:T(8,128)(2,1)S(1)}, u32[]{:S(2)}, u32[]{:S(2)}) %collective-permute-start.23) | collective-permute-done | bytes 131104 | tf_op jit(solution)/shard_map/ppermute | solution.py:66
  115.7 5.0 %collective-permute-done.24 = bf16[64,1024]{1,0:T(8,128)(2,1)S(1)} collective-permute-done((bf16[64,1024]{1,0:T(8,128)(2,1)S(1)}, bf16[64,1024]{1,0:T(8,128)(2,1)S(1)}, u32[]{:S(2)}, u32[]{:S(2)}) %collective-permute-start.24) | collective-permute-done | bytes 131104 | tf_op jit(solution)/shard_map/ppermute | solution.py:66
  125.0 15.8 %collective-permute-done.45 = bf16[64,1024]{1,0:T(8,128)(2,1)S(1)} collective-permute-done((bf16[64,1024]{1,0:T(8,128)(2,1)S(1)}, bf16[64,1024]{1,0:T(8,128)(2,1)S(1)}, u32[]{:S(2)}, u32[]{:S(2)}) %collective-permute-start.45) | collective-permute-done | bytes 131104 | tf_op jit(solution)/shard_map/ppermute | solution.py:66
  140.8 6.7 %collective-permute-done.46 = bf16[64,1024]{1,0:T(8,128)(2,1)S(1)} collective-permute-done((bf16[64,1024]{1,0:T(8,128)(2,1)S(1)}, bf16[64,1024]{1,0:T(8,128)(2,1)S(1)}, u32[]{:S(2)}, u32[]{:S(2)}) %collective-permute-start.46) | collective-permute-done | bytes 131104 | tf_op jit(solution)/shard_map/ppermute | solution.py:66
  163.8 13.0 %collective-permute-start.29 = (bf16[4,8,64,1024]{3,2,1,0:T(8,128)(2,1)}, bf16[4,8,64,1024]{3,2,1,0:T(8,128)(2,1)}, u32[]{:S(2)}, u32[]{:S(2)}) collective-permute-start(bf16[4,8,64,1024]{3,2,1,0:T(8,128)(2,1)} %get-tuple-element.18), channel_id=1, source_target_pairs={{0,4},{4,0},{1,5},{5,1},{2,6},{6,2},{3,7},{7,3},{8,12},{12,8},{9,1... | collective-permute-start | bytes 12582920 | tf_op jit(solution)/shard_map/ppermute | solution.py:53
  181.9 5.7 %collective-permute-done.49 = bf16[4,64,1024]{2,1,0:T(8,128)(2,1)S(1)} collective-permute-done((bf16[4,64,1024]{2,1,0:T(8,128)(2,1)S(1)}, bf16[4,64,1024]{2,1,0:T(8,128)(2,1)S(1)}, u32[]{:S(2)}, u32[]{:S(2)}) %collective-permute-start.49) | collective-permute-done | bytes 524320 | tf_op jit(solution)/shard_map/ppermute | solution.py:69
  201.3 5.7 %collective-permute-start.55 = (bf16[8,4,64,1024]{3,2,1,0:T(8,128)(2,1)}, bf16[8,4,64,1024]{3,2,1,0:T(8,128)(2,1)}, u32[]{:S(2)}, u32[]{:S(2)}) collective-permute-start(bf16[8,4,64,1024]{3,2,1,0:T(8,128)(2,1)} %bitcast_dynamic-update-slice_fusion), channel_id=1, source_target_pairs={{0,4},{4,0},{1,5},{5,1},{2,6},{6,2},{3,7},{7,3},{8,12},{12,8},{9,1... | collective-permute-start | bytes 12582920 | tf_op jit(solution)/shard_map/ppermute | solution.py:53
  207.2 7.6 %pad_maximum_fusion = bf16[2,4,8,64,1024]{4,3,2,1,0:T(8,128)(2,1)} fusion(bf16[1,4,8,64,1024]{4,3,2,1,0:T(8,128)(2,1)} %bitcast.44, bf16[1,4,8,64,1024]{4,3,2,1,0:T(8,128)(2,1)} %get-tuple-element.17), kind=kLoop, calls=%fused_computation.5 | loop fusion | flops 4194304 | bytes 16777216 | tf_op jit(solution)/shard_map/stack | solution.py:162
  214.8 6.0 %fusion.39 = f32[64,4096]{1,0:T(8,128)S(1)} fusion(bf16[4096,1024]{1,0:T(8,128)(2,1)} %bitcast.227, bf16[128,1024]{1,0:T(8,128)(2,1)S(1)} %multiply_convert_fusion.1), kind=kOutput, calls=%fused_computation.168 | convolution fusion | flops 536870912 | bytes 9568256 | tf_op jit(solution)/shard_map/dot_general | solution.py:164
  225.6 7.5 %pad_maximum_fusion.1 = bf16[2,8,4,64,1024]{4,3,2,1,0:T(8,128)(2,1)} fusion(bf16[1,8,4,64,1024]{4,3,2,1,0:T(8,128)(2,1)} %bitcast.81, bf16[1,8,4,64,1024]{4,3,2,1,0:T(8,128)(2,1)} %bitcast.80), kind=kLoop, calls=%fused_computation.6 | loop fusion | flops 4194304 | bytes 16777216 | tf_op jit(solution)/shard_map/stack | solution.py:161
  242.5 5.5 %select_reduce_fusion.1 = f32[64,4096]{1,0:T(8,128)S(1)} fusion(f32[31,64]{1,0:T(8,128)S(1)} %get-tuple-element.38, s32[31,64]{1,0:T(8,128)S(1)} %bitcast.252), kind=kLoop, calls=%fused_computation.1 | loop fusion | flops 24117248 | bytes 1064448 | tf_op jit(solution)/shard_map/reduce_sum | solution.py:184
  263.3 6.1 %collective-permute-done.41 = f32[4,64,62]{1,2,0:T(8,128)S(1)} collective-permute-done((f32[4,64,62]{1,2,0:T(8,128)S(1)}, f32[4,64,62]{1,2,0:T(8,128)S(1)}, u32[]{:S(2)}, u32[]{:S(2)}) %collective-permute-start.41) | collective-permute-done | bytes 63520 | tf_op jit(solution)/shard_map/ppermute | solution.py:66
  269.4 5.8 %collective-permute-done.42 = f32[4,64,62]{1,2,0:T(8,128)S(1)} collective-permute-done((f32[4,64,62]{1,2,0:T(8,128)S(1)}, f32[4,64,62]{1,2,0:T(8,128)S(1)}, u32[]{:S(2)}, u32[]{:S(2)}) %collective-permute-start.42) | collective-permute-done | bytes 63520 | tf_op jit(solution)/shard_map/ppermute | solution.py:66
  275.9 7.9 %collective-permute-start.43 = (f32[8,4,64,62]{2,0,3,1:T(8,128)S(1)}, f32[8,4,64,62]{2,0,3,1:T(8,128)S(1)}, u32[]{:S(2)}, u32[]{:S(2)}) collective-permute-start(f32[8,4,64,62]{2,0,3,1:T(8,128)S(1)} %copy.97), channel_id=1, source_target_pairs={{0,4},{4,0},{1,5},{5,1},{2,6},{6,2},{3,7},{7,3},{8,12},{12,8},{9,1... | collective-permute-start | bytes 1523720 | tf_op jit(solution)/shard_map/ppermute | solution.py:53
  318.4 5.8 %collective-permute-done.61 = bf16[128,1024]{1,0:T(8,128)(2,1)S(1)} collective-permute-done((bf16[128,1024]{1,0:T(8,128)(2,1)S(1)}, bf16[128,1024]{1,0:T(8,128)(2,1)S(1)}, u32[]{:S(2)}, u32[]{:S(2)}) %collective-permute-start.61) | collective-permute-done | bytes 262176 | tf_op jit(solution)/shard_map/ppermute | solution.py:30
  334.5 7.1 %collective-permute-done.62 = f32[4,8,64,512]{3,2,1,0:T(8,128)} collective-permute-done((f32[4,8,64,512]{3,2,1,0:T(8,128)}, f32[4,8,64,512]{3,2,1,0:T(8,128)}, u32[]{:S(2)}, u32[]{:S(2)}) %collective-permute-start.62) | collective-permute-done | bytes 4194336 | tf_op jit(solution)/shard_map/ppermute | solution.py:97
  349.0 11.6 %collective-permute-done.63 = f32[4,64,512]{2,1,0:T(8,128)S(1)} collective-permute-done((f32[4,64,512]{2,1,0:T(8,128)S(1)}, f32[4,64,512]{2,1,0:T(8,128)S(1)}, u32[]{:S(2)}, u32[]{:S(2)}) %collective-permute-start.63) | collective-permute-done | bytes 524320 | tf_op jit(solution)/shard_map/ppermute | solution.py:102
  360.8 13.4 %collective-permute-done.64 = f32[4,64,512]{2,1,0:T(8,128)S(1)} collective-permute-done((f32[4,64,512]{2,1,0:T(8,128)S(1)}, f32[4,64,512]{2,1,0:T(8,128)S(1)}, u32[]{:S(2)}, u32[]{:S(2)}) %collective-permute-start.64) | collective-permute-done | bytes 524320 | tf_op jit(solution)/shard_map/ppermute | solution.py:102
  377.2 9.9 %collective-permute-done.65 = f32[4,64,512]{2,1,0:T(8,128)S(1)} collective-permute-done((f32[4,64,512]{2,1,0:T(8,128)S(1)}, f32[4,64,512]{2,1,0:T(8,128)S(1)}, u32[]{:S(2)}, u32[]{:S(2)}) %collective-permute-start.65) | collective-permute-done | bytes 524320 | tf_op jit(solution)/shard_map/ppermute | solution.py:102
  413.6 9.8 %collective-permute-start.83 = (f32[8,4,1024]{2,0,1:T(8,128)S(1)}, f32[8,4,1024]{2,0,1:T(8,128)S(1)}, u32[]{:S(2)}, u32[]{:S(2)}) collective-permute-start(f32[8,4,1024]{2,0,1:T(8,128)S(1)} %dynamic_update_slice.166), channel_id=1, source_target_pairs={{0,4},{4,0},{1,5},{5,1},{2,6},{6,2},{3,7},{7,3},{8,12},{12,8},{9,1... | collective-permute-start | bytes 393224 | tf_op jit(solution)/shard_map/ppermute | solution.py:23
  (312 shorter events, 234.3 us)
Async XLA Ops:
  42.4 12.4 %collective-permute-start.11 = (bf16[4,8,64,512]{3,2,1,0:T(8,128)(2,1)S(1)}, bf16[4,8,64,512]{3,2,1,0:T(8,128)(2,1)}, u32[]{:S(2)}, u32[]{:S(2)}) collective-permute-start(bf16[4,8,64,512]{3,2,1,0:T(8,128)(2,1)S(1)} %fusion.8), channel_id=1, source_target_pairs={{0,4},{4,0},{1,5},{5,1},{2,6},{6,2},{3,7},{7,3},{8,12},{12,8},{9,1... | collective-permute-start | bytes 6291464 | tf_op jit(solution)/shard_map/ppermute | solution.py:23
  61.3 14.7 %collective-permute-start.12 = (f32[128,1024]{1,0:T(8,128)}, f32[128,1024]{1,0:T(8,128)S(1)}, u32[]{:S(2)}, u32[]{:S(2)}) collective-permute-start(f32[128,1024]{1,0:T(8,128)} %bitcast.21), channel_id=1, source_target_pairs={{0,1},{1,2},{2,3},{3,0},{4,5},{5,6},{6,7},{7,4},{8,9},{9,10},{10,1... | collective-permute-start | bytes 1572872 | tf_op jit(solution)/shard_map/ppermute | solution.py:102
  62.8 13.6 %collective-permute-start.14 = (f32[128,1024]{1,0:T(8,128)S(1)}, f32[128,1024]{1,0:T(8,128)}, u32[]{:S(2)}, u32[]{:S(2)}) collective-permute-start(f32[128,1024]{1,0:T(8,128)S(1)} %bitcast.241), channel_id=1, source_target_pairs={{0,3},{1,0},{2,1},{3,2},{4,7},{5,4},{6,5},{7,6},{8,11},{9,8},{10,9... | collective-permute-start | bytes 1572872 | tf_op jit(solution)/shard_map/ppermute | solution.py:108
  76.0 13.6 %collective-permute-start.13 = (f32[128,1024]{1,0:T(8,128)S(1)}, f32[128,1024]{1,0:T(8,128)S(1)}, u32[]{:S(2)}, u32[]{:S(2)}) collective-permute-start(f32[128,1024]{1,0:T(8,128)S(1)} %bitcast_add_fusion.8), channel_id=1, source_target_pairs={{0,1},{1,2},{2,3},{3,0},{4,5},{5,6},{6,7},{7,4},{8,9},{9,10},{10,1... | collective-permute-start | bytes 1572872 | tf_op jit(solution)/shard_map/ppermute | solution.py:102
  120.8 28.4 %collective-permute-start.25 = (bf16[8,64,1024]{2,1,0:T(8,128)(2,1)S(1)}, bf16[8,64,1024]{2,1,0:T(8,128)(2,1)S(1)}, u32[]{:S(2)}, u32[]{:S(2)}) collective-permute-start(bf16[8,64,1024]{2,1,0:T(8,128)(2,1)S(1)} %bitcast_dynamic-update-slice_fusion.18), channel_id=1, source_target_pairs={{0,192},{64,0},{128,64},{192,128},{1,193},{65,1},{129,65},{193,129... | collective-permute-start | bytes 3145736 | tf_op jit(solution)/shard_map/ppermute | solution.py:69
  120.9 28.5 %collective-permute-start.26 = (bf16[8,64,1024]{2,1,0:T(8,128)(2,1)S(1)}, bf16[8,64,1024]{2,1,0:T(8,128)(2,1)S(1)}, u32[]{:S(2)}, u32[]{:S(2)}) collective-permute-start(bf16[8,64,1024]{2,1,0:T(8,128)(2,1)S(1)} %bitcast_dynamic-update-slice_fusion.18), channel_id=1, source_target_pairs={{0,64},{64,128},{128,192},{192,0},{1,65},{65,129},{129,193},{193,1... | collective-permute-start | bytes 3145736 | tf_op jit(solution)/shard_map/ppermute | solution.py:66
  122.3 18.5 %collective-permute-start.45 = (bf16[64,1024]{1,0:T(8,128)(2,1)S(1)}, bf16[64,1024]{1,0:T(8,128)(2,1)S(1)}, u32[]{:S(2)}, u32[]{:S(2)}) collective-permute-start(bf16[64,1024]{1,0:T(8,128)(2,1)S(1)} %get-tuple-element.33), channel_id=1, source_target_pairs={{0,64},{64,128},{128,192},{192,0},{1,65},{65,129},{129,193},{193,1... | collective-permute-start | bytes 393224 | tf_op jit(solution)/shard_map/ppermute | solution.py:66
  122.3 18.5 %collective-permute-start.44 = (bf16[64,1024]{1,0:T(8,128)(2,1)S(1)}, bf16[64,1024]{1,0:T(8,128)(2,1)S(1)}, u32[]{:S(2)}, u32[]{:S(2)}) collective-permute-start(bf16[64,1024]{1,0:T(8,128)(2,1)S(1)} %get-tuple-element.33), channel_id=1, source_target_pairs={{0,192},{64,0},{128,64},{192,128},{1,193},{65,1},{129,65},{193,129... | collective-permute-start | bytes 393224 | tf_op jit(solution)/shard_map/ppermute | solution.py:69
  155.8 21.1 %collective-permute-start.48 = (bf16[4,64,1024]{2,1,0:T(8,128)(2,1)S(1)}, bf16[4,64,1024]{2,1,0:T(8,128)(2,1)S(1)}, u32[]{:S(2)}, u32[]{:S(2)}) collective-permute-start(bf16[4,64,1024]{2,1,0:T(8,128)(2,1)S(1)} %collective-permute-done.47), channel_id=1, source_target_pairs={{0,56},{8,0},{16,8},{24,16},{32,24},{40,32},{48,40},{56,48},{1,57}... | collective-permute-start | bytes 1572872 | tf_op jit(solution)/shard_map/ppermute | solution.py:69
  157.3 22.4 %collective-permute-start.51 = (bf16[4,64,1024]{2,1,0:T(8,128)(2,1)S(1)}, bf16[4,64,1024]{2,1,0:T(8,128)(2,1)S(1)}, u32[]{:S(2)}, u32[]{:S(2)}) collective-permute-start(bf16[4,64,1024]{2,1,0:T(8,128)(2,1)S(1)} %collective-permute-done.50), channel_id=1, source_target_pairs={{0,8},{8,16},{16,24},{24,32},{32,40},{40,48},{48,56},{56,0},{1,9},... | collective-permute-start | bytes 1572872 | tf_op jit(solution)/shard_map/ppermute | solution.py:66
  163.8 43.4 %collective-permute-start.29 = (bf16[4,8,64,1024]{3,2,1,0:T(8,128)(2,1)}, bf16[4,8,64,1024]{3,2,1,0:T(8,128)(2,1)}, u32[]{:S(2)}, u32[]{:S(2)}) collective-permute-start(bf16[4,8,64,1024]{3,2,1,0:T(8,128)(2,1)} %get-tuple-element.18), channel_id=1, source_target_pairs={{0,4},{4,0},{1,5},{5,1},{2,6},{6,2},{3,7},{7,3},{8,12},{12,8},{9,1... | collective-permute-start | bytes 12582920 | tf_op jit(solution)/shard_map/ppermute | solution.py:53
  176.8 10.8 %collective-permute-start.49 = (bf16[4,64,1024]{2,1,0:T(8,128)(2,1)S(1)}, bf16[4,64,1024]{2,1,0:T(8,128)(2,1)S(1)}, u32[]{:S(2)}, u32[]{:S(2)}) collective-permute-start(bf16[4,64,1024]{2,1,0:T(8,128)(2,1)S(1)} %collective-permute-done.48), channel_id=1, source_target_pairs={{0,56},{8,0},{16,8},{24,16},{32,24},{40,32},{48,40},{56,48},{1,57}... | collective-permute-start | bytes 1572872 | tf_op jit(solution)/shard_map/ppermute | solution.py:69
  179.8 11.4 %collective-permute-start.52 = (bf16[4,64,1024]{2,1,0:T(8,128)(2,1)S(1)}, bf16[4,64,1024]{2,1,0:T(8,128)(2,1)S(1)}, u32[]{:S(2)}, u32[]{:S(2)}) collective-permute-start(bf16[4,64,1024]{2,1,0:T(8,128)(2,1)S(1)} %collective-permute-done.51), channel_id=1, source_target_pairs={{0,8},{8,16},{16,24},{24,32},{32,40},{40,48},{48,56},{56,0},{1,9},... | collective-permute-start | bytes 1572872 | tf_op jit(solution)/shard_map/ppermute | solution.py:66
  201.3 24.3 %collective-permute-start.55 = (bf16[8,4,64,1024]{3,2,1,0:T(8,128)(2,1)}, bf16[8,4,64,1024]{3,2,1,0:T(8,128)(2,1)}, u32[]{:S(2)}, u32[]{:S(2)}) collective-permute-start(bf16[8,4,64,1024]{3,2,1,0:T(8,128)(2,1)} %bitcast_dynamic-update-slice_fusion), channel_id=1, source_target_pairs={{0,4},{4,0},{1,5},{5,1},{2,6},{6,2},{3,7},{7,3},{8,12},{12,8},{9,1... | collective-permute-start | bytes 12582920 | tf_op jit(solution)/shard_map/ppermute | solution.py:53
  275.9 12.6 %collective-permute-start.43 = (f32[8,4,64,62]{2,0,3,1:T(8,128)S(1)}, f32[8,4,64,62]{2,0,3,1:T(8,128)S(1)}, u32[]{:S(2)}, u32[]{:S(2)}) collective-permute-start(f32[8,4,64,62]{2,0,3,1:T(8,128)S(1)} %copy.97), channel_id=1, source_target_pairs={{0,4},{4,0},{1,5},{5,1},{2,6},{6,2},{3,7},{7,3},{8,12},{12,8},{9,1... | collective-permute-start | bytes 1523720 | tf_op jit(solution)/shard_map/ppermute | solution.py:53
  330.2 11.4 %collective-permute-start.62 = (f32[4,8,64,512]{3,2,1,0:T(8,128)}, f32[4,8,64,512]{3,2,1,0:T(8,128)}, u32[]{:S(2)}, u32[]{:S(2)}) collective-permute-start(f32[4,8,64,512]{3,2,1,0:T(8,128)} %dynamic-slice_bitcast_fusion), channel_id=1, source_target_pairs={{0,4},{4,0},{1,5},{5,1},{2,6},{6,2},{3,7},{7,3},{8,12},{12,8},{9,1... | collective-permute-start | bytes 12582920 | tf_op jit(solution)/shard_map/ppermute | solution.py:97
  346.2 14.4 %collective-permute-start.63 = (f32[4,64,512]{2,1,0:T(8,128)S(1)}, f32[4,64,512]{2,1,0:T(8,128)S(1)}, u32[]{:S(2)}, u32[]{:S(2)}) collective-permute-start(f32[4,64,512]{2,1,0:T(8,128)S(1)} %get-tuple-element.15), channel_id=1, source_target_pairs={{0,8},{8,16},{16,24},{24,32},{32,40},{40,48},{48,56},{56,0},{1,9},... | collective-permute-start | bytes 1572872 | tf_op jit(solution)/shard_map/ppermute | solution.py:102
  346.3 14.5 %collective-permute-start.67 = (f32[4,64,512]{2,1,0:T(8,128)S(1)}, f32[4,64,512]{2,1,0:T(8,128)S(1)}, u32[]{:S(2)}, u32[]{:S(2)}) collective-permute-start(f32[4,64,512]{2,1,0:T(8,128)S(1)} %get-tuple-element.16), channel_id=1, source_target_pairs={{0,56},{8,0},{16,8},{24,16},{32,24},{40,32},{48,40},{56,48},{1,57}... | collective-permute-start | bytes 1572872 | tf_op jit(solution)/shard_map/ppermute | solution.py:107
  360.7 13.5 %collective-permute-start.64 = (f32[4,64,512]{2,1,0:T(8,128)S(1)}, f32[4,64,512]{2,1,0:T(8,128)S(1)}, u32[]{:S(2)}, u32[]{:S(2)}) collective-permute-start(f32[4,64,512]{2,1,0:T(8,128)S(1)} %bitcast_add_fusion.6), channel_id=1, source_target_pairs={{0,8},{8,16},{16,24},{24,32},{32,40},{40,48},{48,56},{56,0},{1,9},... | collective-permute-start | bytes 1572872 | tf_op jit(solution)/shard_map/ppermute | solution.py:102
  374.5 12.7 %collective-permute-start.65 = (f32[4,64,512]{2,1,0:T(8,128)S(1)}, f32[4,64,512]{2,1,0:T(8,128)S(1)}, u32[]{:S(2)}, u32[]{:S(2)}) collective-permute-start(f32[4,64,512]{2,1,0:T(8,128)S(1)} %get-tuple-element.13), channel_id=1, source_target_pairs={{0,8},{8,16},{16,24},{24,32},{32,40},{40,48},{48,56},{56,0},{1,9},... | collective-permute-start | bytes 1572872 | tf_op jit(solution)/shard_map/ppermute | solution.py:102
  374.6 12.6 %collective-permute-start.68 = (f32[4,64,512]{2,1,0:T(8,128)S(1)}, f32[4,64,512]{2,1,0:T(8,128)S(1)}, u32[]{:S(2)}, u32[]{:S(2)}) collective-permute-start(f32[4,64,512]{2,1,0:T(8,128)S(1)} %get-tuple-element.14), channel_id=1, source_target_pairs={{0,56},{8,0},{16,8},{24,16},{32,24},{40,32},{48,40},{56,48},{1,57}... | collective-permute-start | bytes 1572872 | tf_op jit(solution)/shard_map/ppermute | solution.py:107
  387.4 36.1 %collective-permute-start.69 = (f32[4,64,512]{2,1,0:T(8,128)S(1)}, f32[4,64,512]{2,1,0:T(8,128)S(1)}, u32[]{:S(2)}, u32[]{:S(2)}) collective-permute-start(f32[4,64,512]{2,1,0:T(8,128)S(1)} %get-tuple-element.12), channel_id=1, source_target_pairs={{0,56},{8,0},{16,8},{24,16},{32,24},{40,32},{48,40},{56,48},{1,57}... | collective-permute-start | bytes 1572872 | tf_op jit(solution)/shard_map/ppermute | solution.py:108
  389.8 33.6 %collective-permute-start.66 = (f32[4,64,512]{2,1,0:T(8,128)S(1)}, f32[4,64,512]{2,1,0:T(8,128)S(1)}, u32[]{:S(2)}, u32[]{:S(2)}) collective-permute-start(f32[4,64,512]{2,1,0:T(8,128)S(1)} %get-tuple-element.11), channel_id=1, source_target_pairs={{0,8},{8,16},{16,24},{24,32},{32,40},{40,48},{48,56},{56,0},{1,9},... | collective-permute-start | bytes 1572872 | tf_op jit(solution)/shard_map/ppermute | solution.py:102
  413.6 11.1 %collective-permute-start.83 = (f32[8,4,1024]{2,0,1:T(8,128)S(1)}, f32[8,4,1024]{2,0,1:T(8,128)S(1)}, u32[]{:S(2)}, u32[]{:S(2)}) collective-permute-start(f32[8,4,1024]{2,0,1:T(8,128)S(1)} %dynamic_update_slice.166), channel_id=1, source_target_pairs={{0,4},{4,0},{1,5},{5,1},{2,6},{6,2},{3,7},{7,3},{8,12},{12,8},{9,1... | collective-permute-start | bytes 393224 | tf_op jit(solution)/shard_map/ppermute | solution.py:23
  (68 other events, 565.5 us)
where the time goes:
time: 445 us; the launch traced here: 437 us
  waiting for transfers between devices  208 us (47%)
  starting transfers between devices  133 us (30%)
  other arithmetic  49.6 us (11%)
  local copies, waits for them, and re-layouts  23.2 us (5%)
  matrix products  21.4 us (5%)
    ppermute x8, waiting for transfers between devices, ring_reduce(): acc_f = lax.ppermute(acc_f, name, fwd) + block(me + n_fwd - step)  64.4 us
    ppermute x16, waiting for transfers between devices, ring_blocks(): left = lax.ppermute(left, name, fwd)  50.2 us
    ppermute x19, waiting for transfers between devices, ring_collect(): left = lax.ppermute(left, name, fwd)  40.3 us
    ppermute x12, starting transfers between devices, ring_collect(): right = lax.ppermute(right, name, bwd)  33 us
    ppermute x3, starting transfers between devices, ring_blocks(): return [v, lax.ppermute(v, name, fwd)]  26.6 us
    ppermute x12, waiting for transfers between devices, ring_blocks(): right = lax.ppermute(right, name, bwd)  22 us
    ppermute x2, starting transfers between devices, ring_collect(): pair = jnp.stack([v, lax.ppermute(v, name, fwd)])  18.3 us
    ppermute x12, starting transfers between devices, ring_blocks(): right = lax.ppermute(right, name, bwd)  16.1 us
  transfers between devices with their start and end apart: 84, of which 53 were waited for; matrix products, arithmetic and copies ran while one was open for 13% of the time, Pallas kernels for 0%

commit v1 on v0

--- a/solution.py
+++ b/solution.py
@@ -83,12 +83,14 @@
     return ring_collect(gz, "c", lax.axis_size("c"))
 
 
-def ring_reduce(v, name, n, axis):
+def ring_reduce(v, name, n, axis, flip=False):
     if n == 1:
         return v
     me = lax.axis_index(name)
     fwd = [(i, (i + 1) % n) for i in range(n)]
     bwd = [(i, (i - 1) % n) for i in range(n)]
+    if flip:
+        return ring_reduce_mirror(v, name, n, axis, me, fwd, bwd)
 
     def block(j):
         return lax.dynamic_index_in_dim(v, j % n, axis, keepdims=False)
@@ -109,6 +111,24 @@
     return total
 
 
+def ring_reduce_mirror(v, name, n, axis, me, fwd, bwd):
+    def block(j):
+        return lax.dynamic_index_in_dim(v, j % n, axis, keepdims=False)
+
+    n_long = n // 2
+    n_short = (n - 1) // 2
+    acc_l = block(me - n_long)
+    for step in range(1, n_long + 1):
+        acc_l = lax.ppermute(acc_l, name, bwd) + block(me - n_long + step)
+    total = acc_l
+    if n_short > 0:
+        acc_s = block(me + n_short)
+        for step in range(1, n_short):
+            acc_s = lax.ppermute(acc_s, name, fwd) + block(me + n_short - step)
+        total = total + lax.ppermute(acc_s, name, fwd)
+    return total
+
+
 def ring_sum(v, name):
     return jnp.sum(ring_collect(v, name, lax.axis_size(name)), axis=0)
 
@@ -148,7 +168,15 @@
         rows_a, weight_full, (((1,), (1,)), ((), ())), preferred_element_type=jnp.float32
     )
     n_mp = lax.axis_size("mp")
-    proj = ring_reduce(proj_part.reshape(proj_part.shape[0], n_mp, feats), "mp", n_mp, 1)
+    proj_blocks = proj_part.reshape(proj_part.shape[0], n_mp, feats)
+    half_f = feats // 2
+    proj = jnp.concatenate(
+        [
+            ring_reduce(proj_blocks[:, :, :half_f], "mp", n_mp, 1),
+            ring_reduce(proj_blocks[:, :, half_f:], "mp", n_mp, 1, flip=True),
+        ],
+        axis=1,
+    )
     hidden = resid.reshape(2 * pairs_here, feats).astype(jnp.float32) + proj
     normed = hidden * gain
     squares = ring_sum(jnp.sum(normed * normed, axis=1), "mp")

time: 445 us -> 443 us (level)
  waiting for transfers between devices: 208 us -> 197 us
    ppermute x8, waiting for transfers between devices: 64.4 us -> 40.5 us  [ring_reduce(): acc_f = lax.ppermute(acc_f, name, fwd) + block(me + n_fwd - step)]
    ppermute x0 -> x3, waiting for transfers between devices: none -> 7.92 us  [the longest x2 4.71 us: ring_reduce_mirror(): acc_l = lax.ppermute(acc_l, name, bwd) + block(me - n_long + step)]
    ppermute x0 -> x3, starting transfers between devices: none -> 6.39 us  [the longest x2 6.3 us: ring_reduce_mirror(): acc_l = lax.ppermute(acc_l, name, bwd) + block(me - n_long + step)]
  transfers between devices with their start and end apart: 84 -> 87, of which waited for: 53 -> 52; matrix products, arithmetic and copies ran while one was open for 13% -> 15% of each run, Pallas kernels for 0% -> 0%
where the time goes in v1:
time: 443 us; the launch traced here: 436 us
  waiting for transfers between devices  197 us (44%)
  starting transfers between devices  137 us (31%)
  other arithmetic  51.3 us (12%)
  local copies, waits for them, and re-layouts  26.9 us (6%)
  matrix products  21.4 us (5%)
    ppermute x16, waiting for transfers between devices, ring_blocks(): left = lax.ppermute(left, name, fwd)  52.6 us
    ppermute x8, waiting for transfers between devices, ring_reduce(): acc_f = lax.ppermute(acc_f, name, fwd) + block(me + n_fwd - step)  40.5 us
    ppermute x19, waiting for transfers between devices, ring_collect(): left = lax.ppermute(left, name, fwd)  40.1 us
    ppermute x12, starting transfers between devices, ring_collect(): right = lax.ppermute(right, name, bwd)  33.3 us
    ppermute x3, starting transfers between devices, ring_blocks(): return [v, lax.ppermute(v, name, fwd)]  26.3 us
    ppermute x12, waiting for transfers between devices, ring_blocks(): right = lax.ppermute(right, name, bwd)  22.3 us
    ppermute x2, starting transfers between devices, ring_collect(): pair = jnp.stack([v, lax.ppermute(v, name, fwd)])  17.9 us
    ppermute x12, starting transfers between devices, ring_blocks(): right = lax.ppermute(right, name, bwd)  15 us
  transfers between devices with their start and end apart: 87, of which 52 were waited for; matrix products, arithmetic and copies ran while one was open for 15% of the time, Pallas kernels for 0%

profile of v1, /device:TPU:1, one launch (start us, length us, event | category | flops | bytes accessed | tf_op | source)
XLA Modules:
  0.0 435.7 jit_solution(1168484455737430439)
XLA Ops:
  24.8 5.8 %collective-permute-done.8 = bf16[8,64,512]{2,1,0:T(8,128)(2,1)S(1)} collective-permute-done((bf16[8,64,512]{2,1,0:T(8,128)(2,1)S(1)}, bf16[8,64,512]{2,1,0:T(8,128)(2,1)S(1)}, u32[]{:S(2)}, u32[]{:S(2)}) %collective-permute-start.8) | collective-permute-done | bytes 524320 | tf_op jit(solution)/shard_map/ppermute | solution.py:42
  42.4 8.5 %collective-permute-start.11 = (bf16[4,8,64,512]{3,2,1,0:T(8,128)(2,1)S(1)}, bf16[4,8,64,512]{3,2,1,0:T(8,128)(2,1)}, u32[]{:S(2)}, u32[]{:S(2)}) collective-permute-start(bf16[4,8,64,512]{3,2,1,0:T(8,128)(2,1)S(1)} %fusion.8), channel_id=1, source_target_pairs={{0,4},{4,0},{1,5},{5,1},{2,6},{6,2},{3,7},{7,3},{8,12},{12,8},{9,1... | collective-permute-start | bytes 6291464 | tf_op jit(solution)/shard_map/ppermute | solution.py:23
  64.0 4.7 %collective-permute-done.15 = f32[128,512]{1,0:T(8,128)S(1)} collective-permute-done((f32[128,512]{1,0:T(8,128)S(1)}, f32[128,512]{1,0:T(8,128)S(1)}, u32[]{:S(2)}, u32[]{:S(2)}) %collective-permute-start.15) | collective-permute-done | bytes 262176 | tf_op jit(solution)/shard_map/ppermute | solution.py:122
  102.4 6.3 %collective-permute-done.26 = bf16[64,1024]{1,0:T(8,128)(2,1)S(1)} collective-permute-done((bf16[64,1024]{1,0:T(8,128)(2,1)S(1)}, bf16[64,1024]{1,0:T(8,128)(2,1)S(1)}, u32[]{:S(2)}, u32[]{:S(2)}) %collective-permute-start.26) | collective-permute-done | bytes 131104 | tf_op jit(solution)/shard_map/ppermute | solution.py:66
  108.7 5.4 %collective-permute-done.27 = bf16[64,1024]{1,0:T(8,128)(2,1)S(1)} collective-permute-done((bf16[64,1024]{1,0:T(8,128)(2,1)S(1)}, bf16[64,1024]{1,0:T(8,128)(2,1)S(1)}, u32[]{:S(2)}, u32[]{:S(2)}) %collective-permute-start.27) | collective-permute-done | bytes 131104 | tf_op jit(solution)/shard_map/ppermute | solution.py:66
  118.4 16.8 %collective-permute-done.48 = bf16[64,1024]{1,0:T(8,128)(2,1)S(1)} collective-permute-done((bf16[64,1024]{1,0:T(8,128)(2,1)S(1)}, bf16[64,1024]{1,0:T(8,128)(2,1)S(1)}, u32[]{:S(2)}, u32[]{:S(2)}) %collective-permute-start.48) | collective-permute-done | bytes 131104 | tf_op jit(solution)/shard_map/ppermute | solution.py:66
  135.2 6.7 %collective-permute-done.49 = bf16[64,1024]{1,0:T(8,128)(2,1)S(1)} collective-permute-done((bf16[64,1024]{1,0:T(8,128)(2,1)S(1)}, bf16[64,1024]{1,0:T(8,128)(2,1)S(1)}, u32[]{:S(2)}, u32[]{:S(2)}) %collective-permute-start.49) | collective-permute-done | bytes 131104 | tf_op jit(solution)/shard_map/ppermute | solution.py:66
  145.3 5.2 %collective-permute-done.50 = bf16[4,64,1024]{2,1,0:T(8,128)(2,1)S(1)} collective-permute-done((bf16[4,64,1024]{2,1,0:T(8,128)(2,1)S(1)}, bf16[4,64,1024]{2,1,0:T(8,128)(2,1)S(1)}, u32[]{:S(2)}, u32[]{:S(2)}) %collective-permute-start.50) | collective-permute-done | bytes 524320 | tf_op jit(solution)/shard_map/ppermute | solution.py:69
  158.2 13.2 %collective-permute-start.32 = (bf16[4,8,64,1024]{3,2,1,0:T(8,128)(2,1)}, bf16[4,8,64,1024]{3,2,1,0:T(8,128)(2,1)}, u32[]{:S(2)}, u32[]{:S(2)}) collective-permute-start(bf16[4,8,64,1024]{3,2,1,0:T(8,128)(2,1)} %get-tuple-element.16), channel_id=1, source_target_pairs={{0,4},{4,0},{1,5},{5,1},{2,6},{6,2},{3,7},{7,3},{8,12},{12,8},{9,1... | collective-permute-start | bytes 12582920 | tf_op jit(solution)/shard_map/ppermute | solution.py:53
  175.9 6.3 %collective-permute-done.52 = bf16[4,64,1024]{2,1,0:T(8,128)(2,1)S(1)} collective-permute-done((bf16[4,64,1024]{2,1,0:T(8,128)(2,1)S(1)}, bf16[4,64,1024]{2,1,0:T(8,128)(2,1)S(1)}, u32[]{:S(2)}, u32[]{:S(2)}) %collective-permute-start.52) | collective-permute-done | bytes 524320 | tf_op jit(solution)/shard_map/ppermute | solution.py:69
  195.7 5.6 %collective-permute-start.58 = (bf16[8,4,64,1024]{3,2,1,0:T(8,128)(2,1)}, bf16[8,4,64,1024]{3,2,1,0:T(8,128)(2,1)}, u32[]{:S(2)}, u32[]{:S(2)}) collective-permute-start(bf16[8,4,64,1024]{3,2,1,0:T(8,128)(2,1)} %bitcast_dynamic-update-slice_fusion), channel_id=1, source_target_pairs={{0,4},{4,0},{1,5},{5,1},{2,6},{6,2},{3,7},{7,3},{8,12},{12,8},{9,1... | collective-permute-start | bytes 12582920 | tf_op jit(solution)/shard_map/ppermute | solution.py:53
  201.5 7.6 %pad_maximum_fusion = bf16[2,4,8,64,1024]{4,3,2,1,0:T(8,128)(2,1)} fusion(bf16[1,4,8,64,1024]{4,3,2,1,0:T(8,128)(2,1)} %bitcast.49, bf16[1,4,8,64,1024]{4,3,2,1,0:T(8,128)(2,1)} %get-tuple-element.15), kind=kLoop, calls=%fused_computation.5 | loop fusion | flops 4194304 | bytes 16777216 | tf_op jit(solution)/shard_map/stack | solution.py:190
  209.0 6.0 %fusion.47 = f32[64,4096]{1,0:T(8,128)S(1)} fusion(bf16[4096,1024]{1,0:T(8,128)(2,1)} %bitcast.242, bf16[128,1024]{1,0:T(8,128)(2,1)S(1)} %multiply_convert_fusion.1), kind=kOutput, calls=%fused_computation.185 | convolution fusion | flops 536870912 | bytes 9568256 | tf_op jit(solution)/shard_map/dot_general | solution.py:192
  222.4 7.5 %pad_maximum_fusion.1 = bf16[2,8,4,64,1024]{4,3,2,1,0:T(8,128)(2,1)} fusion(bf16[1,8,4,64,1024]{4,3,2,1,0:T(8,128)(2,1)} %bitcast.87, bf16[1,8,4,64,1024]{4,3,2,1,0:T(8,128)(2,1)} %bitcast.86), kind=kLoop, calls=%fused_computation.6 | loop fusion | flops 4194304 | bytes 16777216 | tf_op jit(solution)/shard_map/stack | solution.py:189
  237.0 5.5 %select_reduce_fusion.1 = f32[64,4096]{1,0:T(8,128)S(1)} fusion(f32[31,64]{1,0:T(8,128)S(1)} %get-tuple-element.40, s32[31,64]{1,0:T(8,128)S(1)} %bitcast.280), kind=kLoop, calls=%fused_computation.1 | loop fusion | flops 24117248 | bytes 1064448 | tf_op jit(solution)/shard_map/reduce_sum | solution.py:212
  257.8 6.1 %collective-permute-done.44 = f32[4,64,62]{1,2,0:T(8,128)S(1)} collective-permute-done((f32[4,64,62]{1,2,0:T(8,128)S(1)}, f32[4,64,62]{1,2,0:T(8,128)S(1)}, u32[]{:S(2)}, u32[]{:S(2)}) %collective-permute-start.44) | collective-permute-done | bytes 63520 | tf_op jit(solution)/shard_map/ppermute | solution.py:66
  264.1 6.0 %collective-permute-done.45 = f32[4,64,62]{1,2,0:T(8,128)S(1)} collective-permute-done((f32[4,64,62]{1,2,0:T(8,128)S(1)}, f32[4,64,62]{1,2,0:T(8,128)S(1)}, u32[]{:S(2)}, u32[]{:S(2)}) %collective-permute-start.45) | collective-permute-done | bytes 63520 | tf_op jit(solution)/shard_map/ppermute | solution.py:66
  270.7 7.5 %collective-permute-start.46 = (f32[8,4,64,62]{2,0,3,1:T(8,128)S(1)}, f32[8,4,64,62]{2,0,3,1:T(8,128)S(1)}, u32[]{:S(2)}, u32[]{:S(2)}) collective-permute-start(f32[8,4,64,62]{2,0,3,1:T(8,128)S(1)} %copy.121), channel_id=1, source_target_pairs={{0,4},{4,0},{1,5},{5,1},{2,6},{6,2},{3,7},{7,3},{8,12},{12,8},{9,1... | collective-permute-start | bytes 1523720 | tf_op jit(solution)/shard_map/ppermute | solution.py:53
  314.6 4.8 %collective-permute-done.64 = bf16[128,1024]{1,0:T(8,128)(2,1)S(1)} collective-permute-done((bf16[128,1024]{1,0:T(8,128)(2,1)S(1)}, bf16[128,1024]{1,0:T(8,128)(2,1)S(1)}, u32[]{:S(2)}, u32[]{:S(2)}) %collective-permute-start.64) | collective-permute-done | bytes 262176 | tf_op jit(solution)/shard_map/ppermute | solution.py:30
  329.8 7.1 %collective-permute-done.65 = f32[4,8,64,512]{3,2,1,0:T(8,128)} collective-permute-done((f32[4,8,64,512]{3,2,1,0:T(8,128)}, f32[4,8,64,512]{3,2,1,0:T(8,128)}, u32[]{:S(2)}, u32[]{:S(2)}) %collective-permute-start.65) | collective-permute-done | bytes 4194336 | tf_op jit(solution)/shard_map/ppermute | solution.py:99
  344.2 11.6 %collective-permute-done.66 = f32[4,64,512]{2,1,0:T(8,128)S(1)} collective-permute-done((f32[4,64,512]{2,1,0:T(8,128)S(1)}, f32[4,64,512]{2,1,0:T(8,128)S(1)}, u32[]{:S(2)}, u32[]{:S(2)}) %collective-permute-start.66) | collective-permute-done | bytes 524320 | tf_op jit(solution)/shard_map/ppermute | solution.py:104
  356.1 13.4 %collective-permute-done.67 = f32[4,64,512]{2,1,0:T(8,128)S(1)} collective-permute-done((f32[4,64,512]{2,1,0:T(8,128)S(1)}, f32[4,64,512]{2,1,0:T(8,128)S(1)}, u32[]{:S(2)}, u32[]{:S(2)}) %collective-permute-start.67) | collective-permute-done | bytes 524320 | tf_op jit(solution)/shard_map/ppermute | solution.py:104
  372.7 9.7 %collective-permute-done.68 = f32[4,64,512]{2,1,0:T(8,128)S(1)} collective-permute-done((f32[4,64,512]{2,1,0:T(8,128)S(1)}, f32[4,64,512]{2,1,0:T(8,128)S(1)}, u32[]{:S(2)}, u32[]{:S(2)}) %collective-permute-start.68) | collective-permute-done | bytes 524320 | tf_op jit(solution)/shard_map/ppermute | solution.py:104
  412.4 9.4 %collective-permute-start.86 = (f32[8,4,1024]{2,0,1:T(8,128)S(1)}, f32[8,4,1024]{2,0,1:T(8,128)S(1)}, u32[]{:S(2)}, u32[]{:S(2)}) collective-permute-start(f32[8,4,1024]{2,0,1:T(8,128)S(1)} %dynamic_update_slice.166), channel_id=1, source_target_pairs={{0,4},{4,0},{1,5},{5,1},{2,6},{6,2},{3,7},{7,3},{8,12},{12,8},{9,1... | collective-permute-start | bytes 393224 | tf_op jit(solution)/shard_map/ppermute | solution.py:23
  (339 shorter events, 246.9 us)
Async XLA Ops:
  42.4 12.4 %collective-permute-start.11 = (bf16[4,8,64,512]{3,2,1,0:T(8,128)(2,1)S(1)}, bf16[4,8,64,512]{3,2,1,0:T(8,128)(2,1)}, u32[]{:S(2)}, u32[]{:S(2)}) collective-permute-start(bf16[4,8,64,512]{3,2,1,0:T(8,128)(2,1)S(1)} %fusion.8), channel_id=1, source_target_pairs={{0,4},{4,0},{1,5},{5,1},{2,6},{6,2},{3,7},{7,3},{8,12},{12,8},{9,1... | collective-permute-start | bytes 6291464 | tf_op jit(solution)/shard_map/ppermute | solution.py:23
  63.8 13.9 %collective-permute-start.17 = (f32[128,512]{1,0:T(8,128)S(1)}, f32[128,512]{1,0:T(8,128)S(1)}, u32[]{:S(2)}, u32[]{:S(2)}) collective-permute-start(f32[128,512]{1,0:T(8,128)S(1)} %bitcast.275), channel_id=1, source_target_pairs={{0,1},{1,2},{2,3},{3,0},{4,5},{5,6},{6,7},{7,4},{8,9},{9,10},{10,1... | collective-permute-start | bytes 786440 | tf_op jit(solution)/shard_map/ppermute | solution.py:128
  72.6 10.6 %collective-permute-start.13 = (f32[128,512]{1,0:T(8,128)S(1)}, f32[128,512]{1,0:T(8,128)S(1)}, u32[]{:S(2)}, u32[]{:S(2)}) collective-permute-start(f32[128,512]{1,0:T(8,128)S(1)} %bitcast_add_fusion.10), channel_id=1, source_target_pairs={{0,1},{1,2},{2,3},{3,0},{4,5},{5,6},{6,7},{7,4},{8,9},{9,10},{10,1... | collective-permute-start | bytes 786440 | tf_op jit(solution)/shard_map/ppermute | solution.py:104
  114.2 29.4 %collective-permute-start.28 = (bf16[8,64,1024]{2,1,0:T(8,128)(2,1)S(1)}, bf16[8,64,1024]{2,1,0:T(8,128)(2,1)S(1)}, u32[]{:S(2)}, u32[]{:S(2)}) collective-permute-start(bf16[8,64,1024]{2,1,0:T(8,128)(2,1)S(1)} %bitcast_dynamic-update-slice_fusion.18), channel_id=1, source_target_pairs={{0,192},{64,0},{128,64},{192,128},{1,193},{65,1},{129,65},{193,129... | collective-permute-start | bytes 3145736 | tf_op jit(solution)/shard_map/ppermute | solution.py:69
  114.3 29.4 %collective-permute-start.29 = (bf16[8,64,1024]{2,1,0:T(8,128)(2,1)S(1)}, bf16[8,64,1024]{2,1,0:T(8,128)(2,1)S(1)}, u32[]{:S(2)}, u32[]{:S(2)}) collective-permute-start(bf16[8,64,1024]{2,1,0:T(8,128)(2,1)S(1)} %bitcast_dynamic-update-slice_fusion.18), channel_id=1, source_target_pairs={{0,64},{64,128},{128,192},{192,0},{1,65},{65,129},{129,193},{193,1... | collective-permute-start | bytes 3145736 | tf_op jit(solution)/shard_map/ppermute | solution.py:66
  115.7 19.5 %collective-permute-start.48 = (bf16[64,1024]{1,0:T(8,128)(2,1)S(1)}, bf16[64,1024]{1,0:T(8,128)(2,1)S(1)}, u32[]{:S(2)}, u32[]{:S(2)}) collective-permute-start(bf16[64,1024]{1,0:T(8,128)(2,1)S(1)} %get-tuple-element.35), channel_id=1, source_target_pairs={{0,64},{64,128},{128,192},{192,0},{1,65},{65,129},{129,193},{193,1... | collective-permute-start | bytes 393224 | tf_op jit(solution)/shard_map/ppermute | solution.py:66
  115.8 19.5 %collective-permute-start.47 = (bf16[64,1024]{1,0:T(8,128)(2,1)S(1)}, bf16[64,1024]{1,0:T(8,128)(2,1)S(1)}, u32[]{:S(2)}, u32[]{:S(2)}) collective-permute-start(bf16[64,1024]{1,0:T(8,128)(2,1)S(1)} %get-tuple-element.35), channel_id=1, source_target_pairs={{0,192},{64,0},{128,64},{192,128},{1,193},{65,1},{129,65},{193,129... | collective-permute-start | bytes 393224 | tf_op jit(solution)/shard_map/ppermute | solution.py:69
  143.8 10.7 %collective-permute-start.30 = (bf16[4,64,1024]{2,1,0:T(8,128)(2,1)S(1)}, bf16[4,64,1024]{2,1,0:T(8,128)(2,1)S(1)}, u32[]{:S(2)}, u32[]{:S(2)}) collective-permute-start(bf16[4,64,1024]{2,1,0:T(8,128)(2,1)S(1)} %slice.80), channel_id=1, source_target_pairs={{0,64},{64,128},{128,192},{192,0},{1,65},{65,129},{129,193},{193,1... | collective-permute-start | bytes 1572872 | tf_op jit(solution)/shard_map/ppermute | solution.py:63
  150.4 20.9 %collective-permute-start.51 = (bf16[4,64,1024]{2,1,0:T(8,128)(2,1)S(1)}, bf16[4,64,1024]{2,1,0:T(8,128)(2,1)S(1)}, u32[]{:S(2)}, u32[]{:S(2)}) collective-permute-start(bf16[4,64,1024]{2,1,0:T(8,128)(2,1)S(1)} %collective-permute-done.50), channel_id=1, source_target_pairs={{0,56},{8,0},{16,8},{24,16},{32,24},{40,32},{48,40},{56,48},{1,57}... | collective-permute-start | bytes 1572872 | tf_op jit(solution)/shard_map/ppermute | solution.py:69
  151.7 22.5 %collective-permute-start.54 = (bf16[4,64,1024]{2,1,0:T(8,128)(2,1)S(1)}, bf16[4,64,1024]{2,1,0:T(8,128)(2,1)S(1)}, u32[]{:S(2)}, u32[]{:S(2)}) collective-permute-start(bf16[4,64,1024]{2,1,0:T(8,128)(2,1)S(1)} %collective-permute-done.53), channel_id=1, source_target_pairs={{0,8},{8,16},{16,24},{24,32},{32,40},{40,48},{48,56},{56,0},{1,9},... | collective-permute-start | bytes 1572872 | tf_op jit(solution)/shard_map/ppermute | solution.py:66
  158.2 43.3 %collective-permute-start.32 = (bf16[4,8,64,1024]{3,2,1,0:T(8,128)(2,1)}, bf16[4,8,64,1024]{3,2,1,0:T(8,128)(2,1)}, u32[]{:S(2)}, u32[]{:S(2)}) collective-permute-start(bf16[4,8,64,1024]{3,2,1,0:T(8,128)(2,1)} %get-tuple-element.16), channel_id=1, source_target_pairs={{0,4},{4,0},{1,5},{5,1},{2,6},{6,2},{3,7},{7,3},{8,12},{12,8},{9,1... | collective-permute-start | bytes 12582920 | tf_op jit(solution)/shard_map/ppermute | solution.py:53
  171.3 10.9 %collective-permute-start.52 = (bf16[4,64,1024]{2,1,0:T(8,128)(2,1)S(1)}, bf16[4,64,1024]{2,1,0:T(8,128)(2,1)S(1)}, u32[]{:S(2)}, u32[]{:S(2)}) collective-permute-start(bf16[4,64,1024]{2,1,0:T(8,128)(2,1)S(1)} %collective-permute-done.51), channel_id=1, source_target_pairs={{0,56},{8,0},{16,8},{24,16},{32,24},{40,32},{48,40},{56,48},{1,57}... | collective-permute-start | bytes 1572872 | tf_op jit(solution)/shard_map/ppermute | solution.py:69
  174.3 11.5 %collective-permute-start.55 = (bf16[4,64,1024]{2,1,0:T(8,128)(2,1)S(1)}, bf16[4,64,1024]{2,1,0:T(8,128)(2,1)S(1)}, u32[]{:S(2)}, u32[]{:S(2)}) collective-permute-start(bf16[4,64,1024]{2,1,0:T(8,128)(2,1)S(1)} %collective-permute-done.54), channel_id=1, source_target_pairs={{0,8},{8,16},{16,24},{24,32},{32,40},{40,48},{48,56},{56,0},{1,9},... | collective-permute-start | bytes 1572872 | tf_op jit(solution)/shard_map/ppermute | solution.py:66
  195.7 26.7 %collective-permute-start.58 = (bf16[8,4,64,1024]{3,2,1,0:T(8,128)(2,1)}, bf16[8,4,64,1024]{3,2,1,0:T(8,128)(2,1)}, u32[]{:S(2)}, u32[]{:S(2)}) collective-permute-start(bf16[8,4,64,1024]{3,2,1,0:T(8,128)(2,1)} %bitcast_dynamic-update-slice_fusion), channel_id=1, source_target_pairs={{0,4},{4,0},{1,5},{5,1},{2,6},{6,2},{3,7},{7,3},{8,12},{12,8},{9,1... | collective-permute-start | bytes 12582920 | tf_op jit(solution)/shard_map/ppermute | solution.py:53
  270.7 12.2 %collective-permute-start.46 = (f32[8,4,64,62]{2,0,3,1:T(8,128)S(1)}, f32[8,4,64,62]{2,0,3,1:T(8,128)S(1)}, u32[]{:S(2)}, u32[]{:S(2)}) collective-permute-start(f32[8,4,64,62]{2,0,3,1:T(8,128)S(1)} %copy.121), channel_id=1, source_target_pairs={{0,4},{4,0},{1,5},{5,1},{2,6},{6,2},{3,7},{7,3},{8,12},{12,8},{9,1... | collective-permute-start | bytes 1523720 | tf_op jit(solution)/shard_map/ppermute | solution.py:53
  325.4 11.5 %collective-permute-start.65 = (f32[4,8,64,512]{3,2,1,0:T(8,128)}, f32[4,8,64,512]{3,2,1,0:T(8,128)}, u32[]{:S(2)}, u32[]{:S(2)}) collective-permute-start(f32[4,8,64,512]{3,2,1,0:T(8,128)} %dynamic-slice_bitcast_fusion), channel_id=1, source_target_pairs={{0,4},{4,0},{1,5},{5,1},{2,6},{6,2},{3,7},{7,3},{8,12},{12,8},{9,1... | collective-permute-start | bytes 12582920 | tf_op jit(solution)/shard_map/ppermute | solution.py:99
  341.5 14.4 %collective-permute-start.66 = (f32[4,64,512]{2,1,0:T(8,128)S(1)}, f32[4,64,512]{2,1,0:T(8,128)S(1)}, u32[]{:S(2)}, u32[]{:S(2)}) collective-permute-start(f32[4,64,512]{2,1,0:T(8,128)S(1)} %get-tuple-element.13), channel_id=1, source_target_pairs={{0,8},{8,16},{16,24},{24,32},{32,40},{40,48},{48,56},{56,0},{1,9},... | collective-permute-start | bytes 1572872 | tf_op jit(solution)/shard_map/ppermute | solution.py:104
  341.6 14.5 %collective-permute-start.70 = (f32[4,64,512]{2,1,0:T(8,128)S(1)}, f32[4,64,512]{2,1,0:T(8,128)S(1)}, u32[]{:S(2)}, u32[]{:S(2)}) collective-permute-start(f32[4,64,512]{2,1,0:T(8,128)S(1)} %get-tuple-element.14), channel_id=1, source_target_pairs={{0,56},{8,0},{16,8},{24,16},{32,24},{40,32},{48,40},{56,48},{1,57}... | collective-permute-start | bytes 1572872 | tf_op jit(solution)/shard_map/ppermute | solution.py:109
  356.0 13.5 %collective-permute-start.67 = (f32[4,64,512]{2,1,0:T(8,128)S(1)}, f32[4,64,512]{2,1,0:T(8,128)S(1)}, u32[]{:S(2)}, u32[]{:S(2)}) collective-permute-start(f32[4,64,512]{2,1,0:T(8,128)S(1)} %bitcast_add_fusion.6), channel_id=1, source_target_pairs={{0,8},{8,16},{16,24},{24,32},{32,40},{40,48},{48,56},{56,0},{1,9},... | collective-permute-start | bytes 1572872 | tf_op jit(solution)/shard_map/ppermute | solution.py:104
  369.8 12.7 %collective-permute-start.68 = (f32[4,64,512]{2,1,0:T(8,128)S(1)}, f32[4,64,512]{2,1,0:T(8,128)S(1)}, u32[]{:S(2)}, u32[]{:S(2)}) collective-permute-start(f32[4,64,512]{2,1,0:T(8,128)S(1)} %get-tuple-element.11), channel_id=1, source_target_pairs={{0,8},{8,16},{16,24},{24,32},{32,40},{40,48},{48,56},{56,0},{1,9},... | collective-permute-start | bytes 1572872 | tf_op jit(solution)/shard_map/ppermute | solution.py:104
  369.8 12.6 %collective-permute-start.71 = (f32[4,64,512]{2,1,0:T(8,128)S(1)}, f32[4,64,512]{2,1,0:T(8,128)S(1)}, u32[]{:S(2)}, u32[]{:S(2)}) collective-permute-start(f32[4,64,512]{2,1,0:T(8,128)S(1)} %get-tuple-element.12), channel_id=1, source_target_pairs={{0,56},{8,0},{16,8},{24,16},{32,24},{40,32},{48,40},{56,48},{1,57}... | collective-permute-start | bytes 1572872 | tf_op jit(solution)/shard_map/ppermute | solution.py:109
  383.7 38.2 %collective-permute-start.72 = (f32[4,64,512]{2,1,0:T(8,128)}, f32[4,64,512]{2,1,0:T(8,128)S(1)}, u32[]{:S(2)}, u32[]{:S(2)}) collective-permute-start(f32[4,64,512]{2,1,0:T(8,128)} %get-tuple-element.10), channel_id=1, source_target_pairs={{0,56},{8,0},{16,8},{24,16},{32,24},{40,32},{48,40},{56,48},{1,57}... | collective-permute-start | bytes 1572872 | tf_op jit(solution)/shard_map/ppermute | solution.py:110
  386.3 35.6 %collective-permute-start.69 = (f32[4,64,512]{2,1,0:T(8,128)}, f32[4,64,512]{2,1,0:T(8,128)S(1)}, u32[]{:S(2)}, u32[]{:S(2)}) collective-permute-start(f32[4,64,512]{2,1,0:T(8,128)} %get-tuple-element.9), channel_id=1, source_target_pairs={{0,8},{8,16},{16,24},{24,32},{32,40},{40,48},{48,56},{56,0},{1,9},... | collective-permute-start | bytes 1572872 | tf_op jit(solution)/shard_map/ppermute | solution.py:104
  412.4 10.8 %collective-permute-start.86 = (f32[8,4,1024]{2,0,1:T(8,128)S(1)}, f32[8,4,1024]{2,0,1:T(8,128)S(1)}, u32[]{:S(2)}, u32[]{:S(2)}) collective-permute-start(f32[8,4,1024]{2,0,1:T(8,128)S(1)} %dynamic_update_slice.166), channel_id=1, source_target_pairs={{0,4},{4,0},{1,5},{5,1},{2,6},{6,2},{3,7},{7,3},{8,12},{12,8},{9,1... | collective-permute-start | bytes 393224 | tf_op jit(solution)/shard_map/ppermute | solution.py:23
  (72 other events, 593.0 us)

commit v2 on v1

--- a/solution.py
+++ b/solution.py
@@ -229,6 +229,7 @@
     wg_part = lax.dot_general(
         dh_full, rows_a, (((0,), (0,)), ((), ())), preferred_element_type=jnp.float32
     ).reshape(n_x, n_z, n_c, w_rows, heads)
+    gain_grad, wg_part = lax.optimization_barrier((gain_grad, wg_part))
     wg_xz = ring_reduce(wg_part, "c", n_c, 2)
     wg_x = ring_reduce(wg_xz, "z", n_z, 1)
     weight_grad = ring_reduce(wg_x, "x", n_x, 0)

time: 443 us -> 447 us (level)
  the two profiles are of different devices: /device:TPU:1 before, /device:TPU:0 now
where the time goes in v2:
time: 447 us; the launch traced here: 440 us
  waiting for transfers between devices  238 us (53%)
  starting transfers between devices  104 us (23%)
  other arithmetic  50.2 us (11%)
  local copies, waits for them, and re-layouts  23.2 us (5%)
  matrix products  22.4 us (5%)
    ppermute x16, waiting for transfers between devices, ring_blocks(): left = lax.ppermute(left, name, fwd)  57.7 us
    ppermute x19, waiting for transfers between devices, ring_collect(): left = lax.ppermute(left, name, fwd)  47.9 us
    ppermute x8, waiting for transfers between devices, ring_reduce(): acc_f = lax.ppermute(acc_f, name, fwd) + block(me + n_fwd - step)  47.9 us
    ppermute x12, starting transfers between devices, ring_collect(): right = lax.ppermute(right, name, bwd)  39.5 us
    ppermute x12, waiting for transfers between devices, ring_blocks(): right = lax.ppermute(right, name, bwd)  30.6 us
    ppermute x12, starting transfers between devices, ring_blocks(): right = lax.ppermute(right, name, bwd)  19.3 us
    dot_general x3, matrix products, mm(): return jnp.dot(a, b, preferred_element_type=jnp.float32)  13.9 us
    ppermute x16, starting transfers between devices, ring_blocks(): left = lax.ppermute(left, name, fwd)  12.2 us
  transfers between devices with their start and end apart: 87, of which 57 were waited for; matrix products, arithmetic and copies ran while one was open for 14% of the time, Pallas kernels for 0%

profile of v2, /device:TPU:0, one launch (start us, length us, event | category | flops | bytes accessed | tf_op | source)
XLA Modules:
  0.0 440.1 jit_solution(7585560079748816907)
XLA Ops:
  18.3 5.4 %collective-permute-done.6 = bf16[64,512]{1,0:T(8,128)(2,1)S(1)} collective-permute-done((bf16[64,512]{1,0:T(8,128)(2,1)S(1)}, bf16[64,512]{1,0:T(8,128)(2,1)S(1)}, u32[]{:S(2)}, u32[]{:S(2)}) %collective-permute-start.6) | collective-permute-done | bytes 65568 | tf_op jit(solution)/shard_map/ppermute | solution.py:30
  26.9 8.8 %collective-permute-done.8 = bf16[8,64,512]{2,1,0:T(8,128)(2,1)S(1)} collective-permute-done((bf16[8,64,512]{2,1,0:T(8,128)(2,1)S(1)}, bf16[8,64,512]{2,1,0:T(8,128)(2,1)S(1)}, u32[]{:S(2)}, u32[]{:S(2)}) %collective-permute-start.8) | collective-permute-done | bytes 524320 | tf_op jit(solution)/shard_map/ppermute | solution.py:42
  106.3 6.3 %collective-permute-done.26 = bf16[64,1024]{1,0:T(8,128)(2,1)S(1)} collective-permute-done((bf16[64,1024]{1,0:T(8,128)(2,1)S(1)}, bf16[64,1024]{1,0:T(8,128)(2,1)S(1)}, u32[]{:S(2)}, u32[]{:S(2)}) %collective-permute-start.26) | collective-permute-done | bytes 131104 | tf_op jit(solution)/shard_map/ppermute | solution.py:66
  112.6 6.2 %collective-permute-done.27 = bf16[64,1024]{1,0:T(8,128)(2,1)S(1)} collective-permute-done((bf16[64,1024]{1,0:T(8,128)(2,1)S(1)}, bf16[64,1024]{1,0:T(8,128)(2,1)S(1)}, u32[]{:S(2)}, u32[]{:S(2)}) %collective-permute-start.27) | collective-permute-done | bytes 131104 | tf_op jit(solution)/shard_map/ppermute | solution.py:66
  124.2 18.0 %collective-permute-done.48 = bf16[64,1024]{1,0:T(8,128)(2,1)S(1)} collective-permute-done((bf16[64,1024]{1,0:T(8,128)(2,1)S(1)}, bf16[64,1024]{1,0:T(8,128)(2,1)S(1)}, u32[]{:S(2)}, u32[]{:S(2)}) %collective-permute-start.48) | collective-permute-done | bytes 131104 | tf_op jit(solution)/shard_map/ppermute | solution.py:66
  142.6 7.1 %collective-permute-done.49 = bf16[64,1024]{1,0:T(8,128)(2,1)S(1)} collective-permute-done((bf16[64,1024]{1,0:T(8,128)(2,1)S(1)}, bf16[64,1024]{1,0:T(8,128)(2,1)S(1)}, u32[]{:S(2)}, u32[]{:S(2)}) %collective-permute-start.49) | collective-permute-done | bytes 131104 | tf_op jit(solution)/shard_map/ppermute | solution.py:66
  154.2 7.4 %collective-permute-done.50 = bf16[4,64,1024]{2,1,0:T(8,128)(2,1)S(1)} collective-permute-done((bf16[4,64,1024]{2,1,0:T(8,128)(2,1)S(1)}, bf16[4,64,1024]{2,1,0:T(8,128)(2,1)S(1)}, u32[]{:S(2)}, u32[]{:S(2)}) %collective-permute-start.50) | collective-permute-done | bytes 524320 | tf_op jit(solution)/shard_map/ppermute | solution.py:69
  176.5 6.7 %collective-permute-done.52 = bf16[4,64,1024]{2,1,0:T(8,128)(2,1)S(1)} collective-permute-done((bf16[4,64,1024]{2,1,0:T(8,128)(2,1)S(1)}, bf16[4,64,1024]{2,1,0:T(8,128)(2,1)S(1)}, u32[]{:S(2)}, u32[]{:S(2)}) %collective-permute-start.52) | collective-permute-done | bytes 524320 | tf_op jit(solution)/shard_map/ppermute | solution.py:69
  198.3 7.6 %pad_maximum_fusion = bf16[2,4,8,64,1024]{4,3,2,1,0:T(8,128)(2,1)} fusion(bf16[1,4,8,64,1024]{4,3,2,1,0:T(8,128)(2,1)} %bitcast.49, bf16[1,4,8,64,1024]{4,3,2,1,0:T(8,128)(2,1)} %get-tuple-element.19), kind=kLoop, calls=%fused_computation.5 | loop fusion | flops 4194304 | bytes 16777216 | tf_op jit(solution)/shard_map/stack | solution.py:190
  205.9 6.0 %fusion.47 = f32[64,4096]{1,0:T(8,128)S(1)} fusion(bf16[4096,1024]{1,0:T(8,128)(2,1)} %bitcast.242, bf16[128,1024]{1,0:T(8,128)(2,1)S(1)} %multiply_convert_fusion.1), kind=kOutput, calls=%fused_computation.185 | convolution fusion | flops 536870912 | bytes 9568256 | tf_op jit(solution)/shard_map/dot_general | solution.py:192
  219.7 7.5 %pad_maximum_fusion.1 = bf16[2,8,4,64,1024]{4,3,2,1,0:T(8,128)(2,1)} fusion(bf16[1,8,4,64,1024]{4,3,2,1,0:T(8,128)(2,1)} %bitcast.87, bf16[1,8,4,64,1024]{4,3,2,1,0:T(8,128)(2,1)} %bitcast.86), kind=kLoop, calls=%fused_computation.6 | loop fusion | flops 4194304 | bytes 16777216 | tf_op jit(solution)/shard_map/stack | solution.py:189
  227.3 4.9 %collective-permute-done.35 = f32[64,32]{0,1:T(8,128)S(1)} collective-permute-done((f32[64,32]{0,1:T(8,128)S(1)}, f32[64,32]{0,1:T(8,128)S(1)}, u32[]{:S(2)}, u32[]{:S(2)}) %collective-permute-start.35) | collective-permute-done | bytes 8224 | tf_op jit(solution)/shard_map/ppermute | solution.py:30
  236.0 5.5 %select_reduce_fusion.1 = f32[64,4096]{1,0:T(8,128)S(1)} fusion(f32[31,64]{1,0:T(8,128)S(1)} %get-tuple-element.44, s32[31,64]{1,0:T(8,128)S(1)} %bitcast.281), kind=kLoop, calls=%fused_computation.1 | loop fusion | flops 24117248 | bytes 1064448 | tf_op jit(solution)/shard_map/reduce_sum | solution.py:212
  241.7 5.1 %collective-permute-done.38 = f32[64,62]{0,1:T(8,128)S(1)} collective-permute-done((f32[64,62]{0,1:T(8,128)S(1)}, f32[64,62]{0,1:T(8,128)S(1)}, u32[]{:S(2)}, u32[]{:S(2)}) %collective-permute-start.38) | collective-permute-done | bytes 15904 | tf_op jit(solution)/shard_map/ppermute | solution.py:66
  261.0 6.9 %collective-permute-done.44 = f32[4,64,62]{1,2,0:T(8,128)S(1)} collective-permute-done((f32[4,64,62]{1,2,0:T(8,128)S(1)}, f32[4,64,62]{1,2,0:T(8,128)S(1)}, u32[]{:S(2)}, u32[]{:S(2)}) %collective-permute-start.44) | collective-permute-done | bytes 63520 | tf_op jit(solution)/shard_map/ppermute | solution.py:66
  268.1 6.1 %collective-permute-done.45 = f32[4,64,62]{1,2,0:T(8,128)S(1)} collective-permute-done((f32[4,64,62]{1,2,0:T(8,128)S(1)}, f32[4,64,62]{1,2,0:T(8,128)S(1)}, u32[]{:S(2)}, u32[]{:S(2)}) %collective-permute-start.45) | collective-permute-done | bytes 63520 | tf_op jit(solution)/shard_map/ppermute | solution.py:66
  275.0 5.5 %fusion = f32[128,1024]{1,0:T(8,128)} fusion(bf16[4096,1024]{1,0:T(8,128)(2,1)} %bitcast.243, bf16[64,4096]{1,0:T(8,128)(2,1)S(1)} %get-tuple-element.7, bf16[64,4096]{1,0:T(8,128)(2,1)S(1)} %get-tuple-element.8), kind=kOutput, calls=%fused_computation.15 | convolution fusion | flops 1075838976 | bytes 9961472 | tf_op jit(solution)/shard_map/dot_general | solution.py:143
  290.2 4.8 %fusion.4 = f32[128,1024]{1,0:T(8,128)S(1)} fusion(bf16[4096,1024]{1,0:T(8,128)(2,1)} %bitcast.255, bf16[64,4096]{1,0:T(8,128)(2,1)S(1)} %get-tuple-element.9, bf16[64,4096]{1,0:T(8,128)(2,1)S(1)} %get-tuple-element.10), kind=kOutput, calls=%fused_computation.19 | convolution fusion | flops 1075838976 | bytes 9961472 | tf_op jit(solution)/shard_map/dot_general | solution.py:143
  339.5 7.4 %collective-permute-done.64 = bf16[128,1024]{1,0:T(8,128)(2,1)S(1)} collective-permute-done((bf16[128,1024]{1,0:T(8,128)(2,1)S(1)}, bf16[128,1024]{1,0:T(8,128)(2,1)S(1)}, u32[]{:S(2)}, u32[]{:S(2)}) %collective-permute-start.64) | collective-permute-done | bytes 262176 | tf_op jit(solution)/shard_map/ppermute | solution.py:30
  352.9 7.5 %collective-permute-done.76 = f32[4,8,64,512]{3,2,1,0:T(8,128)} collective-permute-done((f32[4,8,64,512]{3,2,1,0:T(8,128)}, f32[4,8,64,512]{3,2,1,0:T(8,128)}, u32[]{:S(2)}, u32[]{:S(2)}) %collective-permute-start.76) | collective-permute-done | bytes 4194336 | tf_op jit(solution)/shard_map/ppermute | solution.py:99
  368.3 12.1 %collective-permute-done.77 = f32[4,64,512]{2,1,0:T(8,128)S(1)} collective-permute-done((f32[4,64,512]{2,1,0:T(8,128)S(1)}, f32[4,64,512]{2,1,0:T(8,128)S(1)}, u32[]{:S(2)}, u32[]{:S(2)}) %collective-permute-start.77) | collective-permute-done | bytes 524320 | tf_op jit(solution)/shard_map/ppermute | solution.py:104
  380.6 14.5 %collective-permute-done.78 = f32[4,64,512]{2,1,0:T(8,128)S(1)} collective-permute-done((f32[4,64,512]{2,1,0:T(8,128)S(1)}, f32[4,64,512]{2,1,0:T(8,128)S(1)}, u32[]{:S(2)}, u32[]{:S(2)}) %collective-permute-start.78) | collective-permute-done | bytes 524320 | tf_op jit(solution)/shard_map/ppermute | solution.py:104
  398.7 10.4 %collective-permute-done.79 = f32[4,64,512]{2,1,0:T(8,128)S(1)} collective-permute-done((f32[4,64,512]{2,1,0:T(8,128)S(1)}, f32[4,64,512]{2,1,0:T(8,128)S(1)}, u32[]{:S(2)}, u32[]{:S(2)}) %collective-permute-start.79) | collective-permute-done | bytes 524320 | tf_op jit(solution)/shard_map/ppermute | solution.py:104
  412.3 8.8 %collective-permute-done.83 = f32[4,64,512]{2,1,0:T(8,128)S(1)} collective-permute-done((f32[4,64,512]{2,1,0:T(8,128)S(1)}, f32[4,64,512]{2,1,0:T(8,128)S(1)}, u32[]{:S(2)}, u32[]{:S(2)}) %collective-permute-start.83) | collective-permute-done | bytes 524320 | tf_op jit(solution)/shard_map/ppermute | solution.py:110
  (339 shorter events, 251.3 us)
Async XLA Ops:
  23.8 12.0 %collective-permute-start.8 = (bf16[8,64,512]{2,1,0:T(8,128)(2,1)S(1)}, bf16[8,64,512]{2,1,0:T(8,128)(2,1)S(1)}, u32[]{:S(2)}, u32[]{:S(2)}) collective-permute-start(bf16[8,64,512]{2,1,0:T(8,128)(2,1)S(1)} %bitcast_dynamic-update-slice_fusion.26), channel_id=1, source_target_pairs={{0,192},{64,0},{128,64},{192,128},{1,193},{65,1},{129,65},{193,129... | collective-permute-start | bytes 1572872 | tf_op jit(solution)/shard_map/ppermute | solution.py:42
  26.6 12.1 %collective-permute-start.7 = (bf16[8,64,512]{2,1,0:T(8,128)(2,1)S(1)}, bf16[8,64,512]{2,1,0:T(8,128)(2,1)}, u32[]{:S(2)}, u32[]{:S(2)}) collective-permute-start(bf16[8,64,512]{2,1,0:T(8,128)(2,1)S(1)} %bitcast_dynamic-update-slice_fusion.26), channel_id=1, source_target_pairs={{0,64},{64,128},{128,192},{192,0},{1,65},{65,129},{129,193},{193,1... | collective-permute-start | bytes 1572872 | tf_op jit(solution)/shard_map/ppermute | solution.py:40
  61.2 15.9 %collective-permute-start.17 = (f32[128,512]{1,0:T(8,128)S(1)}, f32[128,512]{1,0:T(8,128)S(1)}, u32[]{:S(2)}, u32[]{:S(2)}) collective-permute-start(f32[128,512]{1,0:T(8,128)S(1)} %bitcast.276), channel_id=1, source_target_pairs={{0,1},{1,2},{2,3},{3,0},{4,5},{5,6},{6,7},{7,4},{8,9},{9,10},{10,1... | collective-permute-start | bytes 786440 | tf_op jit(solution)/shard_map/ppermute | solution.py:128
  118.9 33.1 %collective-permute-start.28 = (bf16[8,64,1024]{2,1,0:T(8,128)(2,1)S(1)}, bf16[8,64,1024]{2,1,0:T(8,128)(2,1)S(1)}, u32[]{:S(2)}, u32[]{:S(2)}) collective-permute-start(bf16[8,64,1024]{2,1,0:T(8,128)(2,1)S(1)} %bitcast_dynamic-update-slice_fusion.18), channel_id=1, source_target_pairs={{0,192},{64,0},{128,64},{192,128},{1,193},{65,1},{129,65},{193,129... | collective-permute-start | bytes 3145736 | tf_op jit(solution)/shard_map/ppermute | solution.py:69
  118.9 33.1 %collective-permute-start.29 = (bf16[8,64,1024]{2,1,0:T(8,128)(2,1)S(1)}, bf16[8,64,1024]{2,1,0:T(8,128)(2,1)S(1)}, u32[]{:S(2)}, u32[]{:S(2)}) collective-permute-start(bf16[8,64,1024]{2,1,0:T(8,128)(2,1)S(1)} %bitcast_dynamic-update-slice_fusion.18), channel_id=1, source_target_pairs={{0,64},{64,128},{128,192},{192,0},{1,65},{65,129},{129,193},{193,1... | collective-permute-start | bytes 3145736 | tf_op jit(solution)/shard_map/ppermute | solution.py:66
  121.0 21.2 %collective-permute-start.48 = (bf16[64,1024]{1,0:T(8,128)(2,1)S(1)}, bf16[64,1024]{1,0:T(8,128)(2,1)S(1)}, u32[]{:S(2)}, u32[]{:S(2)}) collective-permute-start(bf16[64,1024]{1,0:T(8,128)(2,1)S(1)} %get-tuple-element.39), channel_id=1, source_target_pairs={{0,64},{64,128},{128,192},{192,0},{1,65},{65,129},{129,193},{193,1... | collective-permute-start | bytes 393224 | tf_op jit(solution)/shard_map/ppermute | solution.py:66
  121.0 21.6 %collective-permute-start.47 = (bf16[64,1024]{1,0:T(8,128)(2,1)S(1)}, bf16[64,1024]{1,0:T(8,128)(2,1)S(1)}, u32[]{:S(2)}, u32[]{:S(2)}) collective-permute-start(bf16[64,1024]{1,0:T(8,128)(2,1)S(1)} %get-tuple-element.39), channel_id=1, source_target_pairs={{0,192},{64,0},{128,64},{192,128},{1,193},{65,1},{129,65},{193,129... | collective-permute-start | bytes 393224 | tf_op jit(solution)/shard_map/ppermute | solution.py:69
  149.8 11.8 %collective-permute-start.50 = (bf16[4,64,1024]{2,1,0:T(8,128)(2,1)S(1)}, bf16[4,64,1024]{2,1,0:T(8,128)(2,1)S(1)}, u32[]{:S(2)}, u32[]{:S(2)}) collective-permute-start(bf16[4,64,1024]{2,1,0:T(8,128)(2,1)S(1)} %pad_maximum_fusion.5), channel_id=1, source_target_pairs={{0,56},{8,0},{16,8},{24,16},{32,24},{40,32},{48,40},{56,48},{1,57}... | collective-permute-start | bytes 1572872 | tf_op jit(solution)/shard_map/ppermute | solution.py:69
  149.9 14.3 %collective-permute-start.53 = (bf16[4,64,1024]{2,1,0:T(8,128)(2,1)S(1)}, bf16[4,64,1024]{2,1,0:T(8,128)(2,1)S(1)}, u32[]{:S(2)}, u32[]{:S(2)}) collective-permute-start(bf16[4,64,1024]{2,1,0:T(8,128)(2,1)S(1)} %pad_maximum_fusion.5), channel_id=1, source_target_pairs={{0,8},{8,16},{16,24},{24,32},{32,40},{40,48},{48,56},{56,0},{1,9},... | collective-permute-start | bytes 1572872 | tf_op jit(solution)/shard_map/ppermute | solution.py:66
  152.0 12.5 %collective-permute-start.31 = (bf16[4,64,1024]{2,1,0:T(8,128)(2,1)S(1)}, bf16[4,64,1024]{2,1,0:T(8,128)(2,1)S(1)}, u32[]{:S(2)}, u32[]{:S(2)}) collective-permute-start(bf16[4,64,1024]{2,1,0:T(8,128)(2,1)S(1)} %slice.81), channel_id=1, source_target_pairs={{0,192},{64,0},{128,64},{192,128},{1,193},{65,1},{129,65},{193,129... | collective-permute-start | bytes 1572872 | tf_op jit(solution)/shard_map/ppermute | solution.py:63
  152.1 12.3 %collective-permute-start.30 = (bf16[4,64,1024]{2,1,0:T(8,128)(2,1)S(1)}, bf16[4,64,1024]{2,1,0:T(8,128)(2,1)S(1)}, u32[]{:S(2)}, u32[]{:S(2)}) collective-permute-start(bf16[4,64,1024]{2,1,0:T(8,128)(2,1)S(1)} %slice.80), channel_id=1, source_target_pairs={{0,64},{64,128},{128,192},{192,0},{1,65},{65,129},{129,193},{193,1... | collective-permute-start | bytes 1572872 | tf_op jit(solution)/shard_map/ppermute | solution.py:63
  168.1 30.2 %collective-permute-start.32 = (bf16[4,8,64,1024]{3,2,1,0:T(8,128)(2,1)}, bf16[4,8,64,1024]{3,2,1,0:T(8,128)(2,1)}, u32[]{:S(2)}, u32[]{:S(2)}) collective-permute-start(bf16[4,8,64,1024]{3,2,1,0:T(8,128)(2,1)} %get-tuple-element.20), channel_id=1, source_target_pairs={{0,4},{4,0},{1,5},{5,1},{2,6},{6,2},{3,7},{7,3},{8,12},{12,8},{9,1... | collective-permute-start | bytes 12582920 | tf_op jit(solution)/shard_map/ppermute | solution.py:53
  170.9 12.3 %collective-permute-start.52 = (bf16[4,64,1024]{2,1,0:T(8,128)(2,1)S(1)}, bf16[4,64,1024]{2,1,0:T(8,128)(2,1)S(1)}, u32[]{:S(2)}, u32[]{:S(2)}) collective-permute-start(bf16[4,64,1024]{2,1,0:T(8,128)(2,1)S(1)} %collective-permute-done.51), channel_id=1, source_target_pairs={{0,56},{8,0},{16,8},{24,16},{32,24},{40,32},{48,40},{56,48},{1,57}... | collective-permute-start | bytes 1572872 | tf_op jit(solution)/shard_map/ppermute | solution.py:69
  174.8 12.2 %collective-permute-start.55 = (bf16[4,64,1024]{2,1,0:T(8,128)(2,1)S(1)}, bf16[4,64,1024]{2,1,0:T(8,128)(2,1)S(1)}, u32[]{:S(2)}, u32[]{:S(2)}) collective-permute-start(bf16[4,64,1024]{2,1,0:T(8,128)(2,1)S(1)} %collective-permute-done.54), channel_id=1, source_target_pairs={{0,8},{8,16},{16,24},{24,32},{32,40},{40,48},{48,56},{56,0},{1,9},... | collective-permute-start | bytes 1572872 | tf_op jit(solution)/shard_map/ppermute | solution.py:66
  198.0 21.7 %collective-permute-start.58 = (bf16[8,4,64,1024]{3,2,1,0:T(8,128)(2,1)}, bf16[8,4,64,1024]{3,2,1,0:T(8,128)(2,1)}, u32[]{:S(2)}, u32[]{:S(2)}) collective-permute-start(bf16[8,4,64,1024]{3,2,1,0:T(8,128)(2,1)} %bitcast_dynamic-update-slice_fusion), channel_id=1, source_target_pairs={{0,4},{4,0},{1,5},{5,1},{2,6},{6,2},{3,7},{7,3},{8,12},{12,8},{9,1... | collective-permute-start | bytes 12582920 | tf_op jit(solution)/shard_map/ppermute | solution.py:53
  216.4 10.8 %collective-permute-start.33 = (f32[64,32]{0,1:T(8,128)S(1)}, f32[64,32]{0,1:T(8,128)S(1)}, u32[]{:S(2)}, u32[]{:S(2)}) collective-permute-start(f32[64,32]{0,1:T(8,128)S(1)} %get-tuple-element.12), channel_id=1, source_target_pairs={{0,1},{1,2},{2,3},{3,0},{4,5},{5,6},{6,7},{7,4},{8,9},{9,10},{10,1... | collective-permute-start | bytes 24584 | tf_op jit(solution)/shard_map/ppermute | solution.py:40
  216.5 10.8 %collective-permute-start.34 = (f32[64,32]{0,1:T(8,128)S(1)}, f32[64,32]{0,1:T(8,128)S(1)}, u32[]{:S(2)}, u32[]{:S(2)}) collective-permute-start(f32[64,32]{0,1:T(8,128)S(1)} %get-tuple-element.12), channel_id=1, source_target_pairs={{0,3},{1,0},{2,1},{3,2},{4,7},{5,4},{6,5},{7,6},{8,11},{9,8},{10,9... | collective-permute-start | bytes 24584 | tf_op jit(solution)/shard_map/ppermute | solution.py:42
  364.9 15.5 %collective-permute-start.77 = (f32[4,64,512]{2,1,0:T(8,128)S(1)}, f32[4,64,512]{2,1,0:T(8,128)S(1)}, u32[]{:S(2)}, u32[]{:S(2)}) collective-permute-start(f32[4,64,512]{2,1,0:T(8,128)S(1)} %get-tuple-element.17), channel_id=1, source_target_pairs={{0,8},{8,16},{16,24},{24,32},{32,40},{40,48},{48,56},{56,0},{1,9},... | collective-permute-start | bytes 1572872 | tf_op jit(solution)/shard_map/ppermute | solution.py:104
  365.0 15.6 %collective-permute-start.81 = (f32[4,64,512]{2,1,0:T(8,128)S(1)}, f32[4,64,512]{2,1,0:T(8,128)S(1)}, u32[]{:S(2)}, u32[]{:S(2)}) collective-permute-start(f32[4,64,512]{2,1,0:T(8,128)S(1)} %get-tuple-element.18), channel_id=1, source_target_pairs={{0,56},{8,0},{16,8},{24,16},{32,24},{40,32},{48,40},{56,48},{1,57}... | collective-permute-start | bytes 1572872 | tf_op jit(solution)/shard_map/ppermute | solution.py:109
  380.5 14.6 %collective-permute-start.78 = (f32[4,64,512]{2,1,0:T(8,128)S(1)}, f32[4,64,512]{2,1,0:T(8,128)S(1)}, u32[]{:S(2)}, u32[]{:S(2)}) collective-permute-start(f32[4,64,512]{2,1,0:T(8,128)S(1)} %bitcast_add_fusion.6), channel_id=1, source_target_pairs={{0,8},{8,16},{16,24},{24,32},{32,40},{40,48},{48,56},{56,0},{1,9},... | collective-permute-start | bytes 1572872 | tf_op jit(solution)/shard_map/ppermute | solution.py:104
  395.3 13.8 %collective-permute-start.79 = (f32[4,64,512]{2,1,0:T(8,128)S(1)}, f32[4,64,512]{2,1,0:T(8,128)S(1)}, u32[]{:S(2)}, u32[]{:S(2)}) collective-permute-start(f32[4,64,512]{2,1,0:T(8,128)S(1)} %get-tuple-element.15), channel_id=1, source_target_pairs={{0,8},{8,16},{16,24},{24,32},{32,40},{40,48},{48,56},{56,0},{1,9},... | collective-permute-start | bytes 1572872 | tf_op jit(solution)/shard_map/ppermute | solution.py:104
  395.4 13.7 %collective-permute-start.82 = (f32[4,64,512]{2,1,0:T(8,128)S(1)}, f32[4,64,512]{2,1,0:T(8,128)S(1)}, u32[]{:S(2)}, u32[]{:S(2)}) collective-permute-start(f32[4,64,512]{2,1,0:T(8,128)S(1)} %get-tuple-element.16), channel_id=1, source_target_pairs={{0,56},{8,0},{16,8},{24,16},{32,24},{40,32},{48,40},{56,48},{1,57}... | collective-permute-start | bytes 1572872 | tf_op jit(solution)/shard_map/ppermute | solution.py:109
  409.3 11.9 %collective-permute-start.83 = (f32[4,64,512]{2,1,0:T(8,128)S(1)}, f32[4,64,512]{2,1,0:T(8,128)S(1)}, u32[]{:S(2)}, u32[]{:S(2)}) collective-permute-start(f32[4,64,512]{2,1,0:T(8,128)S(1)} %get-tuple-element.14), channel_id=1, source_target_pairs={{0,56},{8,0},{16,8},{24,16},{32,24},{40,32},{48,40},{56,48},{1,57}... | collective-permute-start | bytes 1572872 | tf_op jit(solution)/shard_map/ppermute | solution.py:110
  412.3 12.3 %collective-permute-start.80 = (f32[4,64,512]{2,1,0:T(8,128)S(1)}, f32[4,64,512]{2,1,0:T(8,128)S(1)}, u32[]{:S(2)}, u32[]{:S(2)}) collective-permute-start(f32[4,64,512]{2,1,0:T(8,128)S(1)} %get-tuple-element.13), channel_id=1, source_target_pairs={{0,8},{8,16},{16,24},{24,32},{32,40},{40,48},{48,56},{56,0},{1,9},... | collective-permute-start | bytes 1572872 | tf_op jit(solution)/shard_map/ppermute | solution.py:104
  (72 other events, 628.1 us)

commit v3 on v1

--- a/solution.py
+++ b/solution.py
@@ -230,7 +230,14 @@
         dh_full, rows_a, (((0,), (0,)), ((), ())), preferred_element_type=jnp.float32
     ).reshape(n_x, n_z, n_c, w_rows, heads)
     wg_xz = ring_reduce(wg_part, "c", n_c, 2)
-    wg_x = ring_reduce(wg_xz, "z", n_z, 1)
+    half_h = heads // 2
+    wg_x = jnp.concatenate(
+        [
+            ring_reduce(wg_xz[..., :half_h], "z", n_z, 1),
+            ring_reduce(wg_xz[..., half_h:], "z", n_z, 1, flip=True),
+        ],
+        axis=-1,
+    )
     weight_grad = ring_reduce(wg_x, "x", n_x, 0)
     return (attn_grad, weight_grad, gain_grad)
 

time: 443 us -> 429 us (0.968)
  waiting for transfers between devices: 197 us -> 167 us
  other arithmetic: 51.3 us -> 59.1 us
  starting transfers between devices: 137 us -> 144 us
    ppermute x8, waiting for transfers between devices: 40.5 us -> 12.1 us  [ring_reduce(): acc_f = lax.ppermute(acc_f, name, fwd) + block(me + n_fwd - step)]
    ppermute x2 -> x6, starting transfers between devices: 6.3 us -> 11.1 us  [ring_reduce_mirror(): acc_l = lax.ppermute(acc_l, name, bwd) + block(me - n_long + step)]
  transfers between devices with their start and end apart: 87 -> 94, of which waited for: 52 -> 49; matrix products, arithmetic and copies ran while one was open for 15% -> 17% of each run, Pallas kernels for 0% -> 0%
where the time goes in v3:
time: 429 us; the launch traced here: 421 us
  waiting for transfers between devices  167 us (39%)
  starting transfers between devices  144 us (34%)
  other arithmetic  59.1 us (14%)
  local copies, waits for them, and re-layouts  29 us (7%)
  matrix products  20.2 us (5%)
    ppermute x16, waiting for transfers between devices, ring_blocks(): left = lax.ppermute(left, name, fwd)  53.1 us
    ppermute x19, waiting for transfers between devices, ring_collect(): left = lax.ppermute(left, name, fwd)  36.5 us
    ppermute x12, starting transfers between devices, ring_collect(): right = lax.ppermute(right, name, bwd)  32.1 us
    ppermute x3, starting transfers between devices, ring_blocks(): return [v, lax.ppermute(v, name, fwd)]  26.2 us
    ppermute x12, waiting for transfers between devices, ring_blocks(): right = lax.ppermute(right, name, bwd)  22.3 us
    ppermute x2, starting transfers between devices, ring_collect(): pair = jnp.stack([v, lax.ppermute(v, name, fwd)])  16.9 us
    ppermute x12, starting transfers between devices, ring_blocks(): right = lax.ppermute(right, name, bwd)  15 us
    ppermute x8, waiting for transfers between devices, ring_reduce(): acc_f = lax.ppermute(acc_f, name, fwd) + block(me + n_fwd - step)  12.1 us
  transfers between devices with their start and end apart: 94, of which 49 were waited for; matrix products, arithmetic and copies ran while one was open for 17% of the time, Pallas kernels for 0%

profile of v3, /device:TPU:1, one launch (start us, length us, event | category | flops | bytes accessed | tf_op | source)
XLA Modules:
  0.0 420.6 jit_solution(12307366183776223111)
XLA Ops:
  24.8 5.8 %collective-permute-done.8 = bf16[8,64,512]{2,1,0:T(8,128)(2,1)S(1)} collective-permute-done((bf16[8,64,512]{2,1,0:T(8,128)(2,1)S(1)}, bf16[8,64,512]{2,1,0:T(8,128)(2,1)S(1)}, u32[]{:S(2)}, u32[]{:S(2)}) %collective-permute-start.8) | collective-permute-done | bytes 524320 | tf_op jit(solution)/shard_map/ppermute | solution.py:42
  42.4 8.5 %collective-permute-start.11 = (bf16[4,8,64,512]{3,2,1,0:T(8,128)(2,1)S(1)}, bf16[4,8,64,512]{3,2,1,0:T(8,128)(2,1)}, u32[]{:S(2)}, u32[]{:S(2)}) collective-permute-start(bf16[4,8,64,512]{3,2,1,0:T(8,128)(2,1)S(1)} %fusion.8), channel_id=1, source_target_pairs={{0,4},{4,0},{1,5},{5,1},{2,6},{6,2},{3,7},{7,3},{8,12},{12,8},{9,1... | collective-permute-start | bytes 6291464 | tf_op jit(solution)/shard_map/ppermute | solution.py:23
  64.0 4.7 %collective-permute-done.15 = f32[128,512]{1,0:T(8,128)S(1)} collective-permute-done((f32[128,512]{1,0:T(8,128)S(1)}, f32[128,512]{1,0:T(8,128)S(1)}, u32[]{:S(2)}, u32[]{:S(2)}) %collective-permute-start.15) | collective-permute-done | bytes 262176 | tf_op jit(solution)/shard_map/ppermute | solution.py:122
  102.5 6.3 %collective-permute-done.26 = bf16[64,1024]{1,0:T(8,128)(2,1)S(1)} collective-permute-done((bf16[64,1024]{1,0:T(8,128)(2,1)S(1)}, bf16[64,1024]{1,0:T(8,128)(2,1)S(1)}, u32[]{:S(2)}, u32[]{:S(2)}) %collective-permute-start.26) | collective-permute-done | bytes 131104 | tf_op jit(solution)/shard_map/ppermute | solution.py:66
  108.8 5.4 %collective-permute-done.27 = bf16[64,1024]{1,0:T(8,128)(2,1)S(1)} collective-permute-done((bf16[64,1024]{1,0:T(8,128)(2,1)S(1)}, bf16[64,1024]{1,0:T(8,128)(2,1)S(1)}, u32[]{:S(2)}, u32[]{:S(2)}) %collective-permute-start.27) | collective-permute-done | bytes 131104 | tf_op jit(solution)/shard_map/ppermute | solution.py:66
  118.5 16.8 %collective-permute-done.48 = bf16[64,1024]{1,0:T(8,128)(2,1)S(1)} collective-permute-done((bf16[64,1024]{1,0:T(8,128)(2,1)S(1)}, bf16[64,1024]{1,0:T(8,128)(2,1)S(1)}, u32[]{:S(2)}, u32[]{:S(2)}) %collective-permute-start.48) | collective-permute-done | bytes 131104 | tf_op jit(solution)/shard_map/ppermute | solution.py:66
  135.3 6.7 %collective-permute-done.49 = bf16[64,1024]{1,0:T(8,128)(2,1)S(1)} collective-permute-done((bf16[64,1024]{1,0:T(8,128)(2,1)S(1)}, bf16[64,1024]{1,0:T(8,128)(2,1)S(1)}, u32[]{:S(2)}, u32[]{:S(2)}) %collective-permute-start.49) | collective-permute-done | bytes 131104 | tf_op jit(solution)/shard_map/ppermute | solution.py:66
  145.3 5.2 %collective-permute-done.50 = bf16[4,64,1024]{2,1,0:T(8,128)(2,1)S(1)} collective-permute-done((bf16[4,64,1024]{2,1,0:T(8,128)(2,1)S(1)}, bf16[4,64,1024]{2,1,0:T(8,128)(2,1)S(1)}, u32[]{:S(2)}, u32[]{:S(2)}) %collective-permute-start.50) | collective-permute-done | bytes 524320 | tf_op jit(solution)/shard_map/ppermute | solution.py:69
  158.2 13.2 %collective-permute-start.32 = (bf16[4,8,64,1024]{3,2,1,0:T(8,128)(2,1)}, bf16[4,8,64,1024]{3,2,1,0:T(8,128)(2,1)}, u32[]{:S(2)}, u32[]{:S(2)}) collective-permute-start(bf16[4,8,64,1024]{3,2,1,0:T(8,128)(2,1)} %get-tuple-element.12), channel_id=1, source_target_pairs={{0,4},{4,0},{1,5},{5,1},{2,6},{6,2},{3,7},{7,3},{8,12},{12,8},{9,1... | collective-permute-start | bytes 12582920 | tf_op jit(solution)/shard_map/ppermute | solution.py:53
  176.0 6.3 %collective-permute-done.52 = bf16[4,64,1024]{2,1,0:T(8,128)(2,1)S(1)} collective-permute-done((bf16[4,64,1024]{2,1,0:T(8,128)(2,1)S(1)}, bf16[4,64,1024]{2,1,0:T(8,128)(2,1)S(1)}, u32[]{:S(2)}, u32[]{:S(2)}) %collective-permute-start.52) | collective-permute-done | bytes 524320 | tf_op jit(solution)/shard_map/ppermute | solution.py:69
  195.8 5.5 %collective-permute-start.58 = (bf16[8,4,64,1024]{3,2,1,0:T(8,128)(2,1)}, bf16[8,4,64,1024]{3,2,1,0:T(8,128)(2,1)}, u32[]{:S(2)}, u32[]{:S(2)}) collective-permute-start(bf16[8,4,64,1024]{3,2,1,0:T(8,128)(2,1)} %bitcast_dynamic-update-slice_fusion), channel_id=1, source_target_pairs={{0,4},{4,0},{1,5},{5,1},{2,6},{6,2},{3,7},{7,3},{8,12},{12,8},{9,1... | collective-permute-start | bytes 12582920 | tf_op jit(solution)/shard_map/ppermute | solution.py:53
  201.6 7.6 %pad_maximum_fusion = bf16[2,4,8,64,1024]{4,3,2,1,0:T(8,128)(2,1)} fusion(bf16[1,4,8,64,1024]{4,3,2,1,0:T(8,128)(2,1)} %bitcast.49, bf16[1,4,8,64,1024]{4,3,2,1,0:T(8,128)(2,1)} %get-tuple-element.11), kind=kLoop, calls=%fused_computation.5 | loop fusion | flops 4194304 | bytes 16777216 | tf_op jit(solution)/shard_map/stack | solution.py:190
  209.2 6.1 %fusion.58 = f32[64,4096]{1,0:T(8,128)S(1)} fusion(bf16[4096,1024]{1,0:T(8,128)(2,1)} %bitcast.264, bf16[128,1024]{1,0:T(8,128)(2,1)S(1)} %multiply_convert_fusion.1), kind=kOutput, calls=%fused_computation.208 | convolution fusion | flops 536870912 | bytes 9568256 | tf_op jit(solution)/shard_map/dot_general | solution.py:192
  222.5 7.6 %pad_maximum_fusion.1 = bf16[2,8,4,64,1024]{4,3,2,1,0:T(8,128)(2,1)} fusion(bf16[1,8,4,64,1024]{4,3,2,1,0:T(8,128)(2,1)} %bitcast.87, bf16[1,8,4,64,1024]{4,3,2,1,0:T(8,128)(2,1)} %bitcast.86), kind=kLoop, calls=%fused_computation.6 | loop fusion | flops 4194304 | bytes 16777216 | tf_op jit(solution)/shard_map/stack | solution.py:189
  237.1 5.5 %select_reduce_fusion.1 = f32[64,4096]{1,0:T(8,128)S(1)} fusion(f32[31,64]{1,0:T(8,128)S(1)} %get-tuple-element.48, s32[31,64]{1,0:T(8,128)S(1)} %bitcast.302), kind=kLoop, calls=%fused_computation.1 | loop fusion | flops 24117248 | bytes 1064448 | tf_op jit(solution)/shard_map/reduce_sum | solution.py:212
  257.9 6.1 %collective-permute-done.44 = f32[4,64,62]{1,2,0:T(8,128)S(1)} collective-permute-done((f32[4,64,62]{1,2,0:T(8,128)S(1)}, f32[4,64,62]{1,2,0:T(8,128)S(1)}, u32[]{:S(2)}, u32[]{:S(2)}) %collective-permute-start.44) | collective-permute-done | bytes 63520 | tf_op jit(solution)/shard_map/ppermute | solution.py:66
  264.2 6.0 %collective-permute-done.45 = f32[4,64,62]{1,2,0:T(8,128)S(1)} collective-permute-done((f32[4,64,62]{1,2,0:T(8,128)S(1)}, f32[4,64,62]{1,2,0:T(8,128)S(1)}, u32[]{:S(2)}, u32[]{:S(2)}) %collective-permute-start.45) | collective-permute-done | bytes 63520 | tf_op jit(solution)/shard_map/ppermute | solution.py:66
  270.8 7.5 %collective-permute-start.46 = (f32[8,4,64,62]{2,0,3,1:T(8,128)S(1)}, f32[8,4,64,62]{2,0,3,1:T(8,128)S(1)}, u32[]{:S(2)}, u32[]{:S(2)}) collective-permute-start(f32[8,4,64,62]{2,0,3,1:T(8,128)S(1)} %copy.121), channel_id=1, source_target_pairs={{0,4},{4,0},{1,5},{5,1},{2,6},{6,2},{3,7},{7,3},{8,12},{12,8},{9,1... | collective-permute-start | bytes 1523720 | tf_op jit(solution)/shard_map/ppermute | solution.py:53
  278.4 5.5 %fusion = f32[128,1024]{1,0:T(8,128)} fusion(bf16[4096,1024]{1,0:T(8,128)(2,1)} %bitcast.265, bf16[64,4096]{1,0:T(8,128)(2,1)S(1)} %get-tuple-element.3, bf16[64,4096]{1,0:T(8,128)(2,1)S(1)} %get-tuple-element.4), kind=kOutput, calls=%fused_computation.15 | convolution fusion | flops 1075838976 | bytes 9961472 | tf_op jit(solution)/shard_map/dot_general | solution.py:143
  293.5 4.7 %fusion.4 = f32[128,1024]{1,0:T(8,128)S(1)} fusion(bf16[4096,1024]{1,0:T(8,128)(2,1)} %bitcast.277, bf16[64,4096]{1,0:T(8,128)(2,1)S(1)} %get-tuple-element.5, bf16[64,4096]{1,0:T(8,128)(2,1)S(1)} %get-tuple-element.6), kind=kOutput, calls=%fused_computation.19 | convolution fusion | flops 1075838976 | bytes 9961472 | tf_op jit(solution)/shard_map/dot_general | solution.py:143
  315.1 4.8 %collective-permute-done.64 = bf16[128,1024]{1,0:T(8,128)(2,1)S(1)} collective-permute-done((bf16[128,1024]{1,0:T(8,128)(2,1)S(1)}, bf16[128,1024]{1,0:T(8,128)(2,1)S(1)}, u32[]{:S(2)}, u32[]{:S(2)}) %collective-permute-start.64) | collective-permute-done | bytes 262176 | tf_op jit(solution)/shard_map/ppermute | solution.py:30
  330.4 7.0 %collective-permute-done.65 = f32[4,8,64,512]{3,2,1,0:T(8,128)} collective-permute-done((f32[4,8,64,512]{3,2,1,0:T(8,128)}, f32[4,8,64,512]{3,2,1,0:T(8,128)}, u32[]{:S(2)}, u32[]{:S(2)}) %collective-permute-start.65) | collective-permute-done | bytes 4194336 | tf_op jit(solution)/shard_map/ppermute | solution.py:99
  337.4 4.5 %bitcast_add_fusion = f32[4,8,64,512]{3,2,1,0:T(8,128)S(1)} fusion(f32[4,8,64,512]{3,2,1,0:T(8,128)} %collective-permute-done.65, f32[4,8,2,64,512]{4,3,2,1,0:T(8,128)} %copy-done.3, s32[]{:T(128)S(6)} %select_n.402), kind=kLoop, calls=%fused_computation.10 | loop fusion | flops 1048576 | bytes 12582916 | tf_op jit(solution)/shard_map/add | solution.py:99
  398.1 8.4 %collective-permute-start.93 = (f32[8,4,1024]{2,0,1:T(8,128)S(1)}, f32[8,4,1024]{2,0,1:T(8,128)S(1)}, u32[]{:S(2)}, u32[]{:S(2)}) collective-permute-start(f32[8,4,1024]{2,0,1:T(8,128)S(1)} %dynamic_update_slice.166), channel_id=1, source_target_pairs={{0,4},{4,0},{1,5},{5,1},{2,6},{6,2},{3,7},{7,3},{8,12},{12,8},{9,1... | collective-permute-start | bytes 393224 | tf_op jit(solution)/shard_map/ppermute | solution.py:23
  (361 shorter events, 252.7 us)
Async XLA Ops:
  42.4 12.4 %collective-permute-start.11 = (bf16[4,8,64,512]{3,2,1,0:T(8,128)(2,1)S(1)}, bf16[4,8,64,512]{3,2,1,0:T(8,128)(2,1)}, u32[]{:S(2)}, u32[]{:S(2)}) collective-permute-start(bf16[4,8,64,512]{3,2,1,0:T(8,128)(2,1)S(1)} %fusion.8), channel_id=1, source_target_pairs={{0,4},{4,0},{1,5},{5,1},{2,6},{6,2},{3,7},{7,3},{8,12},{12,8},{9,1... | collective-permute-start | bytes 6291464 | tf_op jit(solution)/shard_map/ppermute | solution.py:23
  63.8 13.9 %collective-permute-start.17 = (f32[128,512]{1,0:T(8,128)S(1)}, f32[128,512]{1,0:T(8,128)S(1)}, u32[]{:S(2)}, u32[]{:S(2)}) collective-permute-start(f32[128,512]{1,0:T(8,128)S(1)} %bitcast.297), channel_id=1, source_target_pairs={{0,1},{1,2},{2,3},{3,0},{4,5},{5,6},{6,7},{7,4},{8,9},{9,10},{10,1... | collective-permute-start | bytes 786440 | tf_op jit(solution)/shard_map/ppermute | solution.py:128
  114.2 29.4 %collective-permute-start.28 = (bf16[8,64,1024]{2,1,0:T(8,128)(2,1)S(1)}, bf16[8,64,1024]{2,1,0:T(8,128)(2,1)S(1)}, u32[]{:S(2)}, u32[]{:S(2)}) collective-permute-start(bf16[8,64,1024]{2,1,0:T(8,128)(2,1)S(1)} %bitcast_dynamic-update-slice_fusion.18), channel_id=1, source_target_pairs={{0,192},{64,0},{128,64},{192,128},{1,193},{65,1},{129,65},{193,129... | collective-permute-start | bytes 3145736 | tf_op jit(solution)/shard_map/ppermute | solution.py:69
  114.3 29.4 %collective-permute-start.29 = (bf16[8,64,1024]{2,1,0:T(8,128)(2,1)S(1)}, bf16[8,64,1024]{2,1,0:T(8,128)(2,1)S(1)}, u32[]{:S(2)}, u32[]{:S(2)}) collective-permute-start(bf16[8,64,1024]{2,1,0:T(8,128)(2,1)S(1)} %bitcast_dynamic-update-slice_fusion.18), channel_id=1, source_target_pairs={{0,64},{64,128},{128,192},{192,0},{1,65},{65,129},{129,193},{193,1... | collective-permute-start | bytes 3145736 | tf_op jit(solution)/shard_map/ppermute | solution.py:66
  115.8 19.5 %collective-permute-start.48 = (bf16[64,1024]{1,0:T(8,128)(2,1)S(1)}, bf16[64,1024]{1,0:T(8,128)(2,1)S(1)}, u32[]{:S(2)}, u32[]{:S(2)}) collective-permute-start(bf16[64,1024]{1,0:T(8,128)(2,1)S(1)} %get-tuple-element.43), channel_id=1, source_target_pairs={{0,64},{64,128},{128,192},{192,0},{1,65},{65,129},{129,193},{193,1... | collective-permute-start | bytes 393224 | tf_op jit(solution)/shard_map/ppermute | solution.py:66
  115.8 19.5 %collective-permute-start.47 = (bf16[64,1024]{1,0:T(8,128)(2,1)S(1)}, bf16[64,1024]{1,0:T(8,128)(2,1)S(1)}, u32[]{:S(2)}, u32[]{:S(2)}) collective-permute-start(bf16[64,1024]{1,0:T(8,128)(2,1)S(1)} %get-tuple-element.43), channel_id=1, source_target_pairs={{0,192},{64,0},{128,64},{192,128},{1,193},{65,1},{129,65},{193,129... | collective-permute-start | bytes 393224 | tf_op jit(solution)/shard_map/ppermute | solution.py:69
  150.5 20.9 %collective-permute-start.51 = (bf16[4,64,1024]{2,1,0:T(8,128)(2,1)S(1)}, bf16[4,64,1024]{2,1,0:T(8,128)(2,1)S(1)}, u32[]{:S(2)}, u32[]{:S(2)}) collective-permute-start(bf16[4,64,1024]{2,1,0:T(8,128)(2,1)S(1)} %collective-permute-done.50), channel_id=1, source_target_pairs={{0,56},{8,0},{16,8},{24,16},{32,24},{40,32},{48,40},{56,48},{1,57}... | collective-permute-start | bytes 1572872 | tf_op jit(solution)/shard_map/ppermute | solution.py:69
  151.8 22.5 %collective-permute-start.54 = (bf16[4,64,1024]{2,1,0:T(8,128)(2,1)S(1)}, bf16[4,64,1024]{2,1,0:T(8,128)(2,1)S(1)}, u32[]{:S(2)}, u32[]{:S(2)}) collective-permute-start(bf16[4,64,1024]{2,1,0:T(8,128)(2,1)S(1)} %collective-permute-done.53), channel_id=1, source_target_pairs={{0,8},{8,16},{16,24},{24,32},{32,40},{40,48},{48,56},{56,0},{1,9},... | collective-permute-start | bytes 1572872 | tf_op jit(solution)/shard_map/ppermute | solution.py:66
  158.2 43.3 %collective-permute-start.32 = (bf16[4,8,64,1024]{3,2,1,0:T(8,128)(2,1)}, bf16[4,8,64,1024]{3,2,1,0:T(8,128)(2,1)}, u32[]{:S(2)}, u32[]{:S(2)}) collective-permute-start(bf16[4,8,64,1024]{3,2,1,0:T(8,128)(2,1)} %get-tuple-element.12), channel_id=1, source_target_pairs={{0,4},{4,0},{1,5},{5,1},{2,6},{6,2},{3,7},{7,3},{8,12},{12,8},{9,1... | collective-permute-start | bytes 12582920 | tf_op jit(solution)/shard_map/ppermute | solution.py:53
  171.4 10.9 %collective-permute-start.52 = (bf16[4,64,1024]{2,1,0:T(8,128)(2,1)S(1)}, bf16[4,64,1024]{2,1,0:T(8,128)(2,1)S(1)}, u32[]{:S(2)}, u32[]{:S(2)}) collective-permute-start(bf16[4,64,1024]{2,1,0:T(8,128)(2,1)S(1)} %collective-permute-done.51), channel_id=1, source_target_pairs={{0,56},{8,0},{16,8},{24,16},{32,24},{40,32},{48,40},{56,48},{1,57}... | collective-permute-start | bytes 1572872 | tf_op jit(solution)/shard_map/ppermute | solution.py:69
  174.3 11.5 %collective-permute-start.55 = (bf16[4,64,1024]{2,1,0:T(8,128)(2,1)S(1)}, bf16[4,64,1024]{2,1,0:T(8,128)(2,1)S(1)}, u32[]{:S(2)}, u32[]{:S(2)}) collective-permute-start(bf16[4,64,1024]{2,1,0:T(8,128)(2,1)S(1)} %collective-permute-done.54), channel_id=1, source_target_pairs={{0,8},{8,16},{16,24},{24,32},{32,40},{40,48},{48,56},{56,0},{1,9},... | collective-permute-start | bytes 1572872 | tf_op jit(solution)/shard_map/ppermute | solution.py:66
  195.8 26.7 %collective-permute-start.58 = (bf16[8,4,64,1024]{3,2,1,0:T(8,128)(2,1)}, bf16[8,4,64,1024]{3,2,1,0:T(8,128)(2,1)}, u32[]{:S(2)}, u32[]{:S(2)}) collective-permute-start(bf16[8,4,64,1024]{3,2,1,0:T(8,128)(2,1)} %bitcast_dynamic-update-slice_fusion), channel_id=1, source_target_pairs={{0,4},{4,0},{1,5},{5,1},{2,6},{6,2},{3,7},{7,3},{8,12},{12,8},{9,1... | collective-permute-start | bytes 12582920 | tf_op jit(solution)/shard_map/ppermute | solution.py:53
  270.8 13.0 %collective-permute-start.46 = (f32[8,4,64,62]{2,0,3,1:T(8,128)S(1)}, f32[8,4,64,62]{2,0,3,1:T(8,128)S(1)}, u32[]{:S(2)}, u32[]{:S(2)}) collective-permute-start(f32[8,4,64,62]{2,0,3,1:T(8,128)S(1)} %copy.121), channel_id=1, source_target_pairs={{0,4},{4,0},{1,5},{5,1},{2,6},{6,2},{3,7},{7,3},{8,12},{12,8},{9,1... | collective-permute-start | bytes 1523720 | tf_op jit(solution)/shard_map/ppermute | solution.py:53
  325.9 11.4 %collective-permute-start.65 = (f32[4,8,64,512]{3,2,1,0:T(8,128)}, f32[4,8,64,512]{3,2,1,0:T(8,128)}, u32[]{:S(2)}, u32[]{:S(2)}) collective-permute-start(f32[4,8,64,512]{3,2,1,0:T(8,128)} %dynamic-slice_bitcast_fusion), channel_id=1, source_target_pairs={{0,4},{4,0},{1,5},{5,1},{2,6},{6,2},{3,7},{7,3},{8,12},{12,8},{9,1... | collective-permute-start | bytes 12582920 | tf_op jit(solution)/shard_map/ppermute | solution.py:99
  346.4 25.3 %collective-permute-start.70 = (f32[4,64,256]{2,1,0:T(8,128)S(1)}, f32[4,64,256]{2,1,0:T(8,128)}, u32[]{:S(2)}, u32[]{:S(2)}) collective-permute-start(f32[4,64,256]{2,1,0:T(8,128)S(1)} %get-tuple-element.24), channel_id=1, source_target_pairs={{0,56},{8,0},{16,8},{24,16},{32,24},{40,32},{48,40},{56,48},{1,57}... | collective-permute-start | bytes 786440 | tf_op jit(solution)/shard_map/ppermute | solution.py:109
  350.2 17.4 %collective-permute-start.73 = (f32[4,64,256]{2,1,0:T(8,128)S(1)}, f32[4,64,256]{2,1,0:T(8,128)}, u32[]{:S(2)}, u32[]{:S(2)}) collective-permute-start(f32[4,64,256]{2,1,0:T(8,128)S(1)} %get-tuple-element.17), channel_id=1, source_target_pairs={{0,56},{8,0},{16,8},{24,16},{32,24},{40,32},{48,40},{56,48},{1,57}... | collective-permute-start | bytes 786440 | tf_op jit(solution)/shard_map/ppermute | solution.py:122
  355.8 18.3 %collective-permute-start.67 = (f32[4,64,256]{2,1,0:T(8,128)}, f32[4,64,256]{2,1,0:T(8,128)S(1)}, u32[]{:S(2)}, u32[]{:S(2)}) collective-permute-start(f32[4,64,256]{2,1,0:T(8,128)} %bitcast_add_fusion.12), channel_id=1, source_target_pairs={{0,8},{8,16},{16,24},{24,32},{32,40},{40,48},{48,56},{56,0},{1,9},... | collective-permute-start | bytes 786440 | tf_op jit(solution)/shard_map/ppermute | solution.py:104
  379.2 10.9 %collective-permute-start.78 = (f32[4,64,256]{2,1,0:T(8,128)S(1)}, f32[4,64,256]{2,1,0:T(8,128)S(1)}, u32[]{:S(2)}, u32[]{:S(2)}) collective-permute-start(f32[4,64,256]{2,1,0:T(8,128)S(1)} %get-tuple-element.16), channel_id=1, source_target_pairs={{0,8},{8,16},{16,24},{24,32},{32,40},{40,48},{48,56},{56,0},{1,9},... | collective-permute-start | bytes 786440 | tf_op jit(solution)/shard_map/ppermute | solution.py:127
  380.7 11.4 %collective-permute-start.90 = (f32[4,1024]{1,0:T(4,128)S(1)}, f32[4,1024]{1,0:T(4,128)S(1)}, u32[]{:S(2)}, u32[]{:S(2)}) collective-permute-start(f32[4,1024]{1,0:T(4,128)S(1)} %collective-permute-done.88), channel_id=1, source_target_pairs={{0,8},{8,16},{16,24},{24,32},{32,40},{40,48},{48,56},{56,0},{1,9},... | collective-permute-start | bytes 49160 | tf_op jit(solution)/shard_map/ppermute | solution.py:40
  382.0 12.0 %collective-permute-start.91 = (f32[4,1024]{1,0:T(4,128)S(1)}, f32[4,1024]{1,0:T(4,128)S(1)}, u32[]{:S(2)}, u32[]{:S(2)}) collective-permute-start(f32[4,1024]{1,0:T(4,128)S(1)} %collective-permute-done.89), channel_id=1, source_target_pairs={{0,56},{8,0},{16,8},{24,16},{32,24},{40,32},{48,40},{56,48},{1,57}... | collective-permute-start | bytes 49160 | tf_op jit(solution)/shard_map/ppermute | solution.py:42
  384.5 22.0 %collective-permute-start.72 = (f32[4,64,256]{2,1,0:T(8,128)S(1)}, f32[4,64,256]{2,1,0:T(8,128)S(1)}, u32[]{:S(2)}, u32[]{:S(2)}) collective-permute-start(f32[4,64,256]{2,1,0:T(8,128)S(1)} %get-tuple-element.20), channel_id=1, source_target_pairs={{0,56},{8,0},{16,8},{24,16},{32,24},{40,32},{48,40},{56,48},{1,57}... | collective-permute-start | bytes 786440 | tf_op jit(solution)/shard_map/ppermute | solution.py:110
  387.8 18.7 %collective-permute-start.69 = (f32[4,64,256]{2,1,0:T(8,128)S(1)}, f32[4,64,256]{2,1,0:T(8,128)S(1)}, u32[]{:S(2)}, u32[]{:S(2)}) collective-permute-start(f32[4,64,256]{2,1,0:T(8,128)S(1)} %get-tuple-element.19), channel_id=1, source_target_pairs={{0,8},{8,16},{16,24},{24,32},{32,40},{40,48},{48,56},{56,0},{1,9},... | collective-permute-start | bytes 786440 | tf_op jit(solution)/shard_map/ppermute | solution.py:104
  391.2 16.3 %collective-permute-start.79 = (f32[4,64,256]{2,1,0:T(8,128)S(1)}, f32[4,64,256]{2,1,0:T(8,128)S(1)}, u32[]{:S(2)}, u32[]{:S(2)}) collective-permute-start(f32[4,64,256]{2,1,0:T(8,128)S(1)} %get-tuple-element.14), channel_id=1, source_target_pairs={{0,8},{8,16},{16,24},{24,32},{32,40},{40,48},{48,56},{56,0},{1,9},... | collective-permute-start | bytes 786440 | tf_op jit(solution)/shard_map/ppermute | solution.py:128
  392.1 15.4 %collective-permute-start.76 = (f32[4,64,256]{2,1,0:T(8,128)S(1)}, f32[4,64,256]{2,1,0:T(8,128)S(1)}, u32[]{:S(2)}, u32[]{:S(2)}) collective-permute-start(f32[4,64,256]{2,1,0:T(8,128)S(1)} %get-tuple-element.13), channel_id=1, source_target_pairs={{0,56},{8,0},{16,8},{24,16},{32,24},{40,32},{48,40},{56,48},{1,57}... | collective-permute-start | bytes 786440 | tf_op jit(solution)/shard_map/ppermute | solution.py:122
  (80 other events, 649.6 us)
